TPU v7x, 512 devices: a whole 4x8x8 slice. The times are simulated.
512 devices in a mesh: ens: 16 (over z, x_hi), tile: 32 (over y, x_lo, core).
Axes of the slice: x: 4 (x_hi: 2, x_lo: 2; x = x_hi * 2 + x_lo), y: 8, z: 8, core: 2. Of those that a mesh axis runs over, the one named last changes fastest.
Arguments:
- conditioning: bfloat16 [12, 256, 128], P(None, 'tile'), may hold values from -6 to 6
- member_noise: float32 [16, 4, 256, 128], P('ens', None, 'tile'), may hold values from -6 to 6
- reg_in: bfloat16 [3, 3, 12, 128], replicated, may hold values from -1 to 1
- reg_down: bfloat16 [3, 3, 128, 128], replicated, may hold values from -0.25 to 0.25
- reg_low: bfloat16 [3, 3, 128, 128], replicated, may hold values from -0.25 to 0.25
- reg_up: bfloat16 [4, 4, 128, 128], replicated, may hold values from -0.375 to 0.375
- reg_fine: bfloat16 [3, 3, 128, 128], replicated, may hold values from -0.25 to 0.25
- reg_out: bfloat16 [3, 3, 4, 128], replicated, may hold values from -0.3125 to 0.3125
- dif_in: bfloat16 [3, 3, 20, 128], replicated, may hold values from -0.75 to 0.75
- dif_down: bfloat16 [3, 3, 128, 128], replicated, may hold values from -0.25 to 0.25
- dif_low: bfloat16 [3, 3, 128, 128], replicated, may hold values from -0.25 to 0.25
- dif_up: bfloat16 [4, 4, 128, 128], replicated, may hold values from -0.375 to 0.375
- dif_fine: bfloat16 [3, 3, 128, 128], replicated, may hold values from -0.25 to 0.25
- dif_out: bfloat16 [3, 3, 4, 128], replicated, may hold values from -0.3125 to 0.3125
Outputs:
- prediction: float32 [16, 4, 256, 128], P('ens', None, 'tile')
All inputs are finite; a program needn't handle non-finite values.
Results may differ from a plain program's by a relative error of at most 0.015.
Values may be sent and summed in bfloat16 or wider, within the bound.
No kernel may reach another device: no remote copies, remote signals or barrier semaphores. Data moves between devices by JAX's collectives and lax.ppermute only.
A program may use at most 64 MiB of HBM per device.

v0:
```python
import jax
import jax.numpy as jnp
from jax import lax
from jax.sharding import PartitionSpec as P

STEPS = 2
sigma_top = 1.0
sigma_ratio = 0.4
sigma_data = 0.5


def with_halo(cells, sides, width):
    for axis, dim in sides:
        count = lax.axis_size(axis)
        ends = count - 1
        head = lax.slice_in_dim(cells, 0, width, axis=dim)
        tail = lax.slice_in_dim(cells, cells.shape[dim] - width, cells.shape[dim], axis=dim)
        cells = jnp.concatenate(
            [
                lax.ppermute(tail, axis, [(i, (i + 1) % count) for i in range(ends)]),
                cells,
                lax.ppermute(head, axis, [((i + 1) % count, i) for i in range(ends)]),
            ],
            axis=dim,
        )
    return cells


def silu_round(values):
    return jax.nn.silu(values).astype(jnp.bfloat16)


def conv_fields(padded, weight):
    height = padded.shape[1] - 2
    across = padded.shape[2] - 2
    running = None
    for tap_y in range(3):
        for tap_x in range(3):
            window = padded[:, tap_y : tap_y + height, tap_x : tap_x + across]
            tap_term = jnp.einsum(
                "crw,co->rwo", window, weight[tap_y, tap_x], preferred_element_type=jnp.float32
            )
            running = tap_term if running is None else running + tap_term
    return running


def conv_feat(padded, weight, stride):
    count_y = (padded.shape[0] - 3) // stride + 1
    count_x = (padded.shape[1] - 3) // stride + 1
    running = None
    for tap_y in range(3):
        for tap_x in range(3):
            window = padded[
                tap_y : tap_y + stride * (count_y - 1) + 1 : stride,
                tap_x : tap_x + stride * (count_x - 1) + 1 : stride,
            ]
            tap_term = jnp.dot(window, weight[tap_y, tap_x], preferred_element_type=jnp.float32)
            running = tap_term if running is None else running + tap_term
    return running


def conv_out(padded, weight):
    height = padded.shape[0] - 2
    across = padded.shape[1] - 2
    running = None
    for tap_y in range(3):
        for tap_x in range(3):
            window = padded[tap_y : tap_y + height, tap_x : tap_x + across]
            tap_term = jnp.einsum(
                "rwc,oc->orw", window, weight[tap_y, tap_x], preferred_element_type=jnp.float32
            )
            running = tap_term if running is None else running + tap_term
    return running


def up_conv(padded, weight):
    count_y = padded.shape[0] - 2
    count_x = padded.shape[1] - 2
    tap_pairs = (((1, 1), (0, 3)), ((2, 0), (1, 2)))

    def parity(side_y, side_x):
        running = None
        for offset_y, kernel_y in tap_pairs[side_y]:
            for offset_x, kernel_x in tap_pairs[side_x]:
                window = padded[offset_y : offset_y + count_y, offset_x : offset_x + count_x]
                tap_term = jnp.dot(
                    window, weight[kernel_y, kernel_x], preferred_element_type=jnp.float32
                )
                running = tap_term if running is None else running + tap_term
        return running

    upper_rows = jnp.stack([parity(0, 0), parity(0, 1)], axis=2)
    lower_rows = jnp.stack([parity(1, 0), parity(1, 1)], axis=2)
    merged = jnp.stack([upper_rows, lower_rows], axis=1)
    return merged.reshape(2 * count_y, 2 * count_x, merged.shape[-1])


def col_pad(values):
    return jnp.pad(values, ((0, 0), (1, 1), (0, 0)))


def feat_pad(values):
    return col_pad(with_halo(values, (("tile", 0),), 1))


def strip_pad(values):
    return with_halo(values, (("ens", 1), ("tile", 0)), 1)


def lower_each(top_level, down_weight, low_weight, up_weight, pad_fn):
    coarse = silu_round(conv_feat(pad_fn(top_level), down_weight, 2))
    middle = silu_round(conv_feat(pad_fn(coarse), low_weight, 1))
    return up_conv(pad_fn(middle), up_weight)


def network_pass(padded_fields, weights, pad_fn, lower_fn):
    in_weight, down_weight, low_weight, up_weight, fine_weight, out_weight = weights
    top_level = silu_round(conv_fields(padded_fields, in_weight))
    upward = lower_fn(top_level, down_weight, low_weight, up_weight, pad_fn)
    summed = (top_level.astype(jnp.float32) + upward).astype(jnp.bfloat16)
    refined = silu_round(conv_feat(pad_fn(summed), fine_weight, 1))
    return conv_out(pad_fn(refined), out_weight)


def shards(
    conditioning,
    member_noise,
    reg_in,
    reg_down,
    reg_low,
    reg_up,
    reg_fine,
    reg_out,
    dif_in,
    dif_down,
    dif_low,
    dif_up,
    dif_fine,
    dif_out,
):
    grid_cols = conditioning.shape[2]
    reg_weights = (reg_in, reg_down, reg_low, reg_up, reg_fine, reg_out)
    dif_weights = (dif_in, dif_down, dif_low, dif_up, dif_fine, dif_out)
    cond_rows = with_halo(conditioning, (("tile", 1),), 1)
    cond_padded = jnp.pad(cond_rows, ((0, 0), (0, 0), (1, 1)))
    strip_width = grid_cols // lax.axis_size("ens")
    strip_start = lax.axis_index("ens") * strip_width
    strip_input = lax.dynamic_slice_in_dim(cond_padded, strip_start, strip_width + 2, 2)
    mean_strip = network_pass(strip_input, reg_weights, strip_pad, lower_each)
    reg_mean = lax.all_gather(mean_strip, "ens", axis=2, tiled=True)
    mean_input = reg_mean.astype(jnp.bfloat16)
    residual_field = sigma_top * member_noise[0]
    for step_index in range(STEPS):
        sigma_now = sigma_top * sigma_ratio**step_index
        sigma_next = sigma_top * sigma_ratio ** (step_index + 1) if step_index + 1 < STEPS else 0.0
        scale_sq = sigma_now**2 + sigma_data**2
        in_gain = 1.0 / scale_sq**0.5
        skip_gain = sigma_data**2 / scale_sq
        out_gain = sigma_now * sigma_data / scale_sq**0.5
        inputs = jnp.concatenate(
            [(in_gain * residual_field).astype(jnp.bfloat16), conditioning, mean_input], axis=0
        )
        inputs_padded = with_halo(inputs, (("tile", 1),), 1)
        inputs_padded = jnp.pad(inputs_padded, ((0, 0), (0, 0), (1, 1)))
        network = network_pass(inputs_padded, dif_weights, feat_pad, lower_each)
        denoised = skip_gain * residual_field + out_gain * network
        residual_field = residual_field + (sigma_next - sigma_now) / sigma_now * (
            residual_field - denoised
        )
    return (reg_mean + residual_field)[None]


def solution(mesh):
    return jax.shard_map(
        shards,
        mesh=mesh,
        in_specs=(
            P(None, "tile", None),
            P("ens", None, "tile", None),
            P(),
            P(),
            P(),
            P(),
            P(),
            P(),
            P(),
            P(),
            P(),
            P(),
            P(),
            P(),
        ),
        out_specs=P("ens", None, "tile", None),
        check_vma=False,
    )
```

profile of v0, /device:TPU:27, one launch (start us, length us, event | category | flops | bytes accessed | tf_op | source)
XLA Modules:
  0.0 311.5 jit_solution(14510241800380738027)
XLA Ops:
  1.0 2.6 collective-permute-start.1
  3.7 5.1 %collective-permute-start = (bf16[12,1,128]{0,2,1:T(8,128)(2,1)S(1)}, bf16[12,1,128]{0,2,1:T(8,128)(2,1)S(1)}, u32[]{:S(2)}, u32[]{:S(2)}) collective-permute-start(bf16[12,1,128]{0,2,1:T(8,128)(2,1)S(1)} %copy.39), channel_id=1, source_target_pairs={{0,1},{1,2},{2,3},{3,4},{4,5},{5,6},{6,7},{7,8},{8,9},{9,10},{10,1... | collective-permute-start | bytes 9224 | tf_op jit(solution)/shard_map/ppermute | solution.py:20
  11.3 3.7 %collective-permute-start.2 = (bf16[8,1,128]{2,1,0:T(2,128)(2,1)S(1)}, bf16[8,1,128]{2,1,0:T(2,128)(2,1)S(1)}, u32[]{:S(2)}, u32[]{:S(2)}) collective-permute-start(bf16[8,1,128]{2,1,0:T(2,128)(2,1)S(1)} %get-tuple-element.45), channel_id=1, source_target_pairs={{0,32},{32,64},{64,96},{96,128},{128,160},{160,192},{192,224},{224... | collective-permute-start | bytes 6152 | tf_op jit(solution)/shard_map/ppermute | solution.py:20
  17.0 4.0 %collective-permute-done.3 = bf16[8,1,128]{2,1,0:T(2,128)(2,1)S(1)} collective-permute-done((bf16[8,1,128]{2,1,0:T(2,128)(2,1)S(1)}, bf16[8,1,128]{2,1,0:T(2,128)(2,1)S(1)}, u32[]{:S(2)}, u32[]{:S(2)}) %collective-permute-start.3) | collective-permute-done | bytes 2080 | tf_op jit(solution)/shard_map/ppermute | solution.py:22
  21.1 8.4 %collective-permute-start.4 = (bf16[1,10,128]{2,1,0:T(8,128)(2,1)S(1)}, bf16[1,10,128]{2,1,0:T(8,128)(2,1)S(1)}, u32[]{:S(2)}, u32[]{:S(2)}) collective-permute-start(bf16[1,10,128]{2,1,0:T(8,128)(2,1)S(1)} %get-tuple-element.29), channel_id=1, source_target_pairs={{0,1},{1,2},{2,3},{3,4},{4,5},{5,6},{6,7},{7,8},{8,9},{9,10},{10,1... | collective-permute-start | bytes 7688 | tf_op jit(solution)/shard_map/ppermute | solution.py:20
  31.7 4.8 %collective-permute-done.5 = bf16[1,10,128]{2,1,0:T(8,128)(2,1)S(1)} collective-permute-done((bf16[1,10,128]{2,1,0:T(8,128)(2,1)S(1)}, bf16[1,10,128]{2,1,0:T(8,128)(2,1)S(1)}, u32[]{:S(2)}, u32[]{:S(2)}) %collective-permute-start.5) | collective-permute-done | bytes 2592 | tf_op jit(solution)/shard_map/ppermute | solution.py:22
  37.8 4.5 %collective-permute-start.6 = (bf16[4,1,128]{2,1,0:T(2,128)(2,1)S(1)}, bf16[4,1,128]{2,1,0:T(2,128)(2,1)S(1)}, u32[]{:S(2)}, u32[]{:S(2)}) collective-permute-start(bf16[4,1,128]{2,1,0:T(2,128)(2,1)S(1)} %get-tuple-element.57), channel_id=1, source_target_pairs={{0,32},{32,64},{64,96},{96,128},{128,160},{160,192},{192,224},{224... | collective-permute-start | bytes 3080 | tf_op jit(solution)/shard_map/ppermute | solution.py:20
  43.8 4.4 %collective-permute-done.7 = bf16[4,1,128]{2,1,0:T(2,128)(2,1)S(1)} collective-permute-done((bf16[4,1,128]{2,1,0:T(2,128)(2,1)S(1)}, bf16[4,1,128]{2,1,0:T(2,128)(2,1)S(1)}, u32[]{:S(2)}, u32[]{:S(2)}) %collective-permute-start.7) | collective-permute-done | bytes 1056 | tf_op jit(solution)/shard_map/ppermute | solution.py:22
  48.2 4.0 %collective-permute-start.8 = (bf16[1,6,128]{2,1,0:T(8,128)(2,1)S(1)}, bf16[1,6,128]{2,1,0:T(8,128)(2,1)S(1)}, u32[]{:S(2)}, u32[]{:S(2)}) collective-permute-start(bf16[1,6,128]{2,1,0:T(8,128)(2,1)S(1)} %get-tuple-element.53), channel_id=1, source_target_pairs={{0,1},{1,2},{2,3},{3,4},{4,5},{5,6},{6,7},{7,8},{8,9},{9,10},{10,1... | collective-permute-start | bytes 4616 | tf_op jit(solution)/shard_map/ppermute | solution.py:20
  54.2 4.9 %collective-permute-done.9 = bf16[1,6,128]{2,1,0:T(8,128)(2,1)S(1)} collective-permute-done((bf16[1,6,128]{2,1,0:T(8,128)(2,1)S(1)}, bf16[1,6,128]{2,1,0:T(8,128)(2,1)S(1)}, u32[]{:S(2)}, u32[]{:S(2)}) %collective-permute-start.9) | collective-permute-done | bytes 1568 | tf_op jit(solution)/shard_map/ppermute | solution.py:22
  60.6 3.8 %collective-permute-start.10 = (bf16[4,1,128]{2,1,0:T(2,128)(2,1)S(1)}, bf16[4,1,128]{2,1,0:T(2,128)(2,1)S(1)}, u32[]{:S(2)}, u32[]{:S(2)}) collective-permute-start(bf16[4,1,128]{2,1,0:T(2,128)(2,1)S(1)} %get-tuple-element.55), channel_id=1, source_target_pairs={{0,32},{32,64},{64,96},{96,128},{128,160},{160,192},{192,224},{224... | collective-permute-start | bytes 3080 | tf_op jit(solution)/shard_map/ppermute | solution.py:20
  65.8 4.4 %collective-permute-done.11 = bf16[4,1,128]{2,1,0:T(2,128)(2,1)S(1)} collective-permute-done((bf16[4,1,128]{2,1,0:T(2,128)(2,1)S(1)}, bf16[4,1,128]{2,1,0:T(2,128)(2,1)S(1)}, u32[]{:S(2)}, u32[]{:S(2)}) %collective-permute-start.11) | collective-permute-done | bytes 1056 | tf_op jit(solution)/shard_map/ppermute | solution.py:22
  70.2 4.0 %collective-permute-start.12 = (bf16[1,6,128]{2,1,0:T(8,128)(2,1)S(1)}, bf16[1,6,128]{2,1,0:T(8,128)(2,1)S(1)}, u32[]{:S(2)}, u32[]{:S(2)}) collective-permute-start(bf16[1,6,128]{2,1,0:T(8,128)(2,1)S(1)} %get-tuple-element.49), channel_id=1, source_target_pairs={{0,1},{1,2},{2,3},{3,4},{4,5},{5,6},{6,7},{7,8},{8,9},{9,10},{10,1... | collective-permute-start | bytes 4616 | tf_op jit(solution)/shard_map/ppermute | solution.py:20
  76.4 4.8 %collective-permute-done.13 = bf16[1,6,128]{2,1,0:T(8,128)(2,1)S(1)} collective-permute-done((bf16[1,6,128]{2,1,0:T(8,128)(2,1)S(1)}, bf16[1,6,128]{2,1,0:T(8,128)(2,1)S(1)}, u32[]{:S(2)}, u32[]{:S(2)}) %collective-permute-start.13) | collective-permute-done | bytes 1568 | tf_op jit(solution)/shard_map/ppermute | solution.py:22
  82.7 4.5 %collective-permute-start.14 = (bf16[8,1,128]{2,1,0:T(2,128)(2,1)S(1)}, bf16[8,1,128]{2,1,0:T(2,128)(2,1)S(1)}, u32[]{:S(2)}, u32[]{:S(2)}) collective-permute-start(bf16[8,1,128]{2,1,0:T(2,128)(2,1)S(1)} %get-tuple-element.43), channel_id=1, source_target_pairs={{0,32},{32,64},{64,96},{96,128},{128,160},{160,192},{192,224},{224... | collective-permute-start | bytes 6152 | tf_op jit(solution)/shard_map/ppermute | solution.py:20
  88.6 4.4 %collective-permute-done.15 = bf16[8,1,128]{2,1,0:T(2,128)(2,1)S(1)} collective-permute-done((bf16[8,1,128]{2,1,0:T(2,128)(2,1)S(1)}, bf16[8,1,128]{2,1,0:T(2,128)(2,1)S(1)}, u32[]{:S(2)}, u32[]{:S(2)}) %collective-permute-start.15) | collective-permute-done | bytes 2080 | tf_op jit(solution)/shard_map/ppermute | solution.py:22
  93.1 4.0 %collective-permute-start.16 = (bf16[1,10,128]{2,1,0:T(8,128)(2,1)S(1)}, bf16[1,10,128]{2,1,0:T(8,128)(2,1)S(1)}, u32[]{:S(2)}, u32[]{:S(2)}) collective-permute-start(bf16[1,10,128]{2,1,0:T(8,128)(2,1)S(1)} %get-tuple-element.37), channel_id=1, source_target_pairs={{0,1},{1,2},{2,3},{3,4},{4,5},{5,6},{6,7},{7,8},{8,9},{9,10},{10,1... | collective-permute-start | bytes 7688 | tf_op jit(solution)/shard_map/ppermute | solution.py:20
  99.1 5.0 %collective-permute-done.17 = bf16[1,10,128]{2,1,0:T(8,128)(2,1)S(1)} collective-permute-done((bf16[1,10,128]{2,1,0:T(8,128)(2,1)S(1)}, bf16[1,10,128]{2,1,0:T(8,128)(2,1)S(1)}, u32[]{:S(2)}, u32[]{:S(2)}) %collective-permute-start.17) | collective-permute-done | bytes 2592 | tf_op jit(solution)/shard_map/ppermute | solution.py:22
  105.1 3.8 %collective-permute-start.18 = (bf16[8,1,128]{2,1,0:T(2,128)(2,1)S(1)}, bf16[8,1,128]{2,1,0:T(2,128)(2,1)S(1)}, u32[]{:S(2)}, u32[]{:S(2)}) collective-permute-start(bf16[8,1,128]{2,1,0:T(2,128)(2,1)S(1)} %get-tuple-element.41), channel_id=1, source_target_pairs={{0,32},{32,64},{64,96},{96,128},{128,160},{160,192},{192,224},{224... | collective-permute-start | bytes 6152 | tf_op jit(solution)/shard_map/ppermute | solution.py:20
  110.4 4.4 %collective-permute-done.19 = bf16[8,1,128]{2,1,0:T(2,128)(2,1)S(1)} collective-permute-done((bf16[8,1,128]{2,1,0:T(2,128)(2,1)S(1)}, bf16[8,1,128]{2,1,0:T(2,128)(2,1)S(1)}, u32[]{:S(2)}, u32[]{:S(2)}) %collective-permute-start.19) | collective-permute-done | bytes 2080 | tf_op jit(solution)/shard_map/ppermute | solution.py:22
  114.8 4.0 %collective-permute-start.20 = (bf16[1,10,128]{2,1,0:T(8,128)(2,1)S(1)}, bf16[1,10,128]{2,1,0:T(8,128)(2,1)S(1)}, u32[]{:S(2)}, u32[]{:S(2)}) collective-permute-start(bf16[1,10,128]{2,1,0:T(8,128)(2,1)S(1)} %get-tuple-element.33), channel_id=1, source_target_pairs={{0,1},{1,2},{2,3},{3,4},{4,5},{5,6},{6,7},{7,8},{8,9},{9,10},{10,1... | collective-permute-start | bytes 7688 | tf_op jit(solution)/shard_map/ppermute | solution.py:20
  120.9 4.9 %collective-permute-done.21 = bf16[1,10,128]{2,1,0:T(8,128)(2,1)S(1)} collective-permute-done((bf16[1,10,128]{2,1,0:T(8,128)(2,1)S(1)}, bf16[1,10,128]{2,1,0:T(8,128)(2,1)S(1)}, u32[]{:S(2)}, u32[]{:S(2)}) %collective-permute-start.21) | collective-permute-done | bytes 2592 | tf_op jit(solution)/shard_map/ppermute | solution.py:22
  127.2 35.0 %all_gather.3 = f32[4,8,128]{1,0,2:T(4,128)S(1)} all-gather(f32[4,8,8]{1,0,2:T(4,128)S(1)} %copy.43), channel_id=1, replica_groups=mesh['ens'=16,'tile'=32] {'ens'}, dimensions={2}, use_global_device_ids=true | all-gather | bytes 17408 | tf_op jit(solution)/shard_map/all_gather | solution.py:150
  162.4 9.7 %collective-permute-start.22 = (bf16[20,1,128]{2,0,1:T(8,128)(2,1)S(1)}, bf16[20,1,128]{2,0,1:T(8,128)(2,1)S(1)}, u32[]{:S(2)}, u32[]{:S(2)}) collective-permute-start(bf16[20,1,128]{2,0,1:T(8,128)(2,1)S(1)} %get-tuple-element.27), channel_id=1, source_target_pairs={{0,1},{1,2},{2,3},{3,4},{4,5},{5,6},{6,7},{7,8},{8,9},{9,10},{10,1... | collective-permute-start | bytes 15368 | tf_op jit(solution)/shard_map/ppermute | solution.py:20
  172.1 2.1 collective-permute-start.23
  174.2 5.1 %collective-permute-done.23 = bf16[20,1,128]{2,0,1:T(8,128)(2,1)S(1)} collective-permute-done((bf16[20,1,128]{2,0,1:T(8,128)(2,1)S(1)}, bf16[20,1,128]{2,0,1:T(8,128)(2,1)S(1)}, u32[]{:S(2)}, u32[]{:S(2)}) %collective-permute-start.23) | collective-permute-done | bytes 5152 | tf_op jit(solution)/shard_map/ppermute | solution.py:22
  184.4 2.4 collective-permute-start.25
  186.8 4.9 %collective-permute-done.25 = bf16[1,128,128]{2,1,0:T(8,128)(2,1)S(1)} collective-permute-done((bf16[1,128,128]{2,1,0:T(8,128)(2,1)S(1)}, bf16[1,128,128]{2,1,0:T(8,128)(2,1)S(1)}, u32[]{:S(2)}, u32[]{:S(2)}) %collective-permute-start.25) | collective-permute-done | bytes 32800 | tf_op jit(solution)/shard_map/ppermute | solution.py:22
  197.0 2.4 collective-permute-start.27
  199.5 4.7 %collective-permute-done.27 = bf16[1,64,128]{2,1,0:T(8,128)(2,1)S(1)} collective-permute-done((bf16[1,64,128]{2,1,0:T(8,128)(2,1)S(1)}, bf16[1,64,128]{2,1,0:T(8,128)(2,1)S(1)}, u32[]{:S(2)}, u32[]{:S(2)}) %collective-permute-start.27) | collective-permute-done | bytes 16416 | tf_op jit(solution)/shard_map/ppermute | solution.py:22
  208.8 2.4 collective-permute-start.29
  211.3 4.6 %collective-permute-done.29 = bf16[1,64,128]{2,1,0:T(8,128)(2,1)S(1)} collective-permute-done((bf16[1,64,128]{2,1,0:T(8,128)(2,1)S(1)}, bf16[1,64,128]{2,1,0:T(8,128)(2,1)S(1)}, u32[]{:S(2)}, u32[]{:S(2)}) %collective-permute-start.29) | collective-permute-done | bytes 16416 | tf_op jit(solution)/shard_map/ppermute | solution.py:22
  220.5 2.5 collective-permute-start.31
  223.1 4.9 %collective-permute-done.31 = bf16[1,128,128]{2,1,0:T(8,128)(2,1)S(1)} collective-permute-done((bf16[1,128,128]{2,1,0:T(8,128)(2,1)S(1)}, bf16[1,128,128]{2,1,0:T(8,128)(2,1)S(1)}, u32[]{:S(2)}, u32[]{:S(2)}) %collective-permute-start.31) | collective-permute-done | bytes 32800 | tf_op jit(solution)/shard_map/ppermute | solution.py:22
  232.1 2.4 collective-permute-start.33
  234.5 4.9 %collective-permute-done.33 = bf16[1,128,128]{2,1,0:T(8,128)(2,1)S(1)} collective-permute-done((bf16[1,128,128]{2,1,0:T(8,128)(2,1)S(1)}, bf16[1,128,128]{2,1,0:T(8,128)(2,1)S(1)}, u32[]{:S(2)}, u32[]{:S(2)}) %collective-permute-start.33) | collective-permute-done | bytes 32800 | tf_op jit(solution)/shard_map/ppermute | solution.py:22
  243.2 2.6 collective-permute-start.35
  245.8 4.5 %collective-permute-done.35 = bf16[20,1,128]{2,0,1:T(8,128)(2,1)S(1)} collective-permute-done((bf16[20,1,128]{2,0,1:T(8,128)(2,1)S(1)}, bf16[20,1,128]{2,0,1:T(8,128)(2,1)S(1)}, u32[]{:S(2)}, u32[]{:S(2)}) %collective-permute-start.35) | collective-permute-done | bytes 5152 | tf_op jit(solution)/shard_map/ppermute | solution.py:22
  255.3 2.4 collective-permute-start.37
  257.7 4.9 %collective-permute-done.37 = bf16[1,128,128]{2,1,0:T(8,128)(2,1)S(1)} collective-permute-done((bf16[1,128,128]{2,1,0:T(8,128)(2,1)S(1)}, bf16[1,128,128]{2,1,0:T(8,128)(2,1)S(1)}, u32[]{:S(2)}, u32[]{:S(2)}) %collective-permute-start.37) | collective-permute-done | bytes 32800 | tf_op jit(solution)/shard_map/ppermute | solution.py:22
  267.7 2.4 collective-permute-start.39
  270.1 4.7 %collective-permute-done.39 = bf16[1,64,128]{2,1,0:T(8,128)(2,1)S(1)} collective-permute-done((bf16[1,64,128]{2,1,0:T(8,128)(2,1)S(1)}, bf16[1,64,128]{2,1,0:T(8,128)(2,1)S(1)}, u32[]{:S(2)}, u32[]{:S(2)}) %collective-permute-start.39) | collective-permute-done | bytes 16416 | tf_op jit(solution)/shard_map/ppermute | solution.py:22
  278.6 2.4 collective-permute-start.41
  281.1 4.6 %collective-permute-done.41 = bf16[1,64,128]{2,1,0:T(8,128)(2,1)S(1)} collective-permute-done((bf16[1,64,128]{2,1,0:T(8,128)(2,1)S(1)}, bf16[1,64,128]{2,1,0:T(8,128)(2,1)S(1)}, u32[]{:S(2)}, u32[]{:S(2)}) %collective-permute-start.41) | collective-permute-done | bytes 16416 | tf_op jit(solution)/shard_map/ppermute | solution.py:22
  290.3 2.4 collective-permute-start.43
  292.7 4.9 %collective-permute-done.43 = bf16[1,128,128]{2,1,0:T(8,128)(2,1)S(1)} collective-permute-done((bf16[1,128,128]{2,1,0:T(8,128)(2,1)S(1)}, bf16[1,128,128]{2,1,0:T(8,128)(2,1)S(1)}, u32[]{:S(2)}, u32[]{:S(2)}) %collective-permute-start.43) | collective-permute-done | bytes 32800 | tf_op jit(solution)/shard_map/ppermute | solution.py:22
  301.8 2.4 collective-permute-start.45
  304.2 4.9 %collective-permute-done.45 = bf16[1,128,128]{2,1,0:T(8,128)(2,1)S(1)} collective-permute-done((bf16[1,128,128]{2,1,0:T(8,128)(2,1)S(1)}, bf16[1,128,128]{2,1,0:T(8,128)(2,1)S(1)}, u32[]{:S(2)}, u32[]{:S(2)}) %collective-permute-start.45) | collective-permute-done | bytes 32800 | tf_op jit(solution)/shard_map/ppermute | solution.py:22
  (350 shorter events, 79.9 us)
Async XLA Ops:
  1.0 8.1 %collective-permute-start.1 = (bf16[12,1,128]{0,2,1:T(8,128)(2,1)S(1)}, bf16[12,1,128]{0,2,1:T(8,128)(2,1)S(1)}, u32[]{:S(2)}, u32[]{:S(2)}) collective-permute-start(bf16[12,1,128]{0,2,1:T(8,128)(2,1)S(1)} %copy.40), channel_id=1, source_target_pairs={{1,0},{2,1},{3,2},{4,3},{5,4},{6,5},{7,6},{8,7},{9,8},{10,9},{11,1... | collective-permute-start | bytes 9224 | tf_op jit(solution)/shard_map/ppermute | solution.py:22
  3.7 6.1 %collective-permute-start = (bf16[12,1,128]{0,2,1:T(8,128)(2,1)S(1)}, bf16[12,1,128]{0,2,1:T(8,128)(2,1)S(1)}, u32[]{:S(2)}, u32[]{:S(2)}) collective-permute-start(bf16[12,1,128]{0,2,1:T(8,128)(2,1)S(1)} %copy.39), channel_id=1, source_target_pairs={{0,1},{1,2},{2,3},{3,4},{4,5},{5,6},{6,7},{7,8},{8,9},{9,10},{10,1... | collective-permute-start | bytes 9224 | tf_op jit(solution)/shard_map/ppermute | solution.py:20
  11.3 5.6 %collective-permute-start.2 = (bf16[8,1,128]{2,1,0:T(2,128)(2,1)S(1)}, bf16[8,1,128]{2,1,0:T(2,128)(2,1)S(1)}, u32[]{:S(2)}, u32[]{:S(2)}) collective-permute-start(bf16[8,1,128]{2,1,0:T(2,128)(2,1)S(1)} %get-tuple-element.45), channel_id=1, source_target_pairs={{0,32},{32,64},{64,96},{96,128},{128,160},{160,192},{192,224},{224... | collective-permute-start | bytes 6152 | tf_op jit(solution)/shard_map/ppermute | solution.py:20
  15.1 5.9 %collective-permute-start.3 = (bf16[8,1,128]{2,1,0:T(2,128)(2,1)S(1)}, bf16[8,1,128]{2,1,0:T(2,128)(2,1)S(1)}, u32[]{:S(2)}, u32[]{:S(2)}) collective-permute-start(bf16[8,1,128]{2,1,0:T(2,128)(2,1)S(1)} %get-tuple-element.46), channel_id=1, source_target_pairs={{32,0},{64,32},{96,64},{128,96},{160,128},{192,160},{224,192},{256... | collective-permute-start | bytes 6152 | tf_op jit(solution)/shard_map/ppermute | solution.py:22
  21.0 22.6 %copy-start.5 = (bf16[3,3,128,128]{3,2,1,0:T(8,128)(2,1)S(1)}, bf16[3,3,128,128]{3,2,1,0:T(8,128)(2,1)}, u32[]{:S(2)}) copy-start(bf16[3,3,128,128]{3,2,1,0:T(8,128)(2,1)} %param.18) | copy-start | bytes 884740
  21.1 10.6 %collective-permute-start.4 = (bf16[1,10,128]{2,1,0:T(8,128)(2,1)S(1)}, bf16[1,10,128]{2,1,0:T(8,128)(2,1)S(1)}, u32[]{:S(2)}, u32[]{:S(2)}) collective-permute-start(bf16[1,10,128]{2,1,0:T(8,128)(2,1)S(1)} %get-tuple-element.29), channel_id=1, source_target_pairs={{0,1},{1,2},{2,3},{3,4},{4,5},{5,6},{6,7},{7,8},{8,9},{9,10},{10,1... | collective-permute-start | bytes 7688 | tf_op jit(solution)/shard_map/ppermute | solution.py:20
  29.5 7.0 %collective-permute-start.5 = (bf16[1,10,128]{2,1,0:T(8,128)(2,1)S(1)}, bf16[1,10,128]{2,1,0:T(8,128)(2,1)S(1)}, u32[]{:S(2)}, u32[]{:S(2)}) collective-permute-start(bf16[1,10,128]{2,1,0:T(8,128)(2,1)S(1)} %get-tuple-element.30), channel_id=1, source_target_pairs={{1,0},{2,1},{3,2},{4,3},{5,4},{6,5},{7,6},{8,7},{9,8},{10,9},{11,1... | collective-permute-start | bytes 7688 | tf_op jit(solution)/shard_map/ppermute | solution.py:22
  36.6 23.6 %copy-start.4 = (bf16[4,4,128,128]{3,2,1,0:T(8,128)(2,1)S(1)}, bf16[4,4,128,128]{3,2,1,0:T(8,128)(2,1)}, u32[]{:S(2)}) copy-start(bf16[4,4,128,128]{3,2,1,0:T(8,128)(2,1)} %param.19) | copy-start | bytes 1572868
  37.8 6.0 %collective-permute-start.6 = (bf16[4,1,128]{2,1,0:T(2,128)(2,1)S(1)}, bf16[4,1,128]{2,1,0:T(2,128)(2,1)S(1)}, u32[]{:S(2)}, u32[]{:S(2)}) collective-permute-start(bf16[4,1,128]{2,1,0:T(2,128)(2,1)S(1)} %get-tuple-element.57), channel_id=1, source_target_pairs={{0,32},{32,64},{64,96},{96,128},{128,160},{160,192},{192,224},{224... | collective-permute-start | bytes 3080 | tf_op jit(solution)/shard_map/ppermute | solution.py:20
  42.3 5.8 %collective-permute-start.7 = (bf16[4,1,128]{2,1,0:T(2,128)(2,1)S(1)}, bf16[4,1,128]{2,1,0:T(2,128)(2,1)S(1)}, u32[]{:S(2)}, u32[]{:S(2)}) collective-permute-start(bf16[4,1,128]{2,1,0:T(2,128)(2,1)S(1)} %get-tuple-element.58), channel_id=1, source_target_pairs={{32,0},{64,32},{96,64},{128,96},{160,128},{192,160},{224,192},{256... | collective-permute-start | bytes 3080 | tf_op jit(solution)/shard_map/ppermute | solution.py:22
  48.2 6.1 %collective-permute-start.8 = (bf16[1,6,128]{2,1,0:T(8,128)(2,1)S(1)}, bf16[1,6,128]{2,1,0:T(8,128)(2,1)S(1)}, u32[]{:S(2)}, u32[]{:S(2)}) collective-permute-start(bf16[1,6,128]{2,1,0:T(8,128)(2,1)S(1)} %get-tuple-element.53), channel_id=1, source_target_pairs={{0,1},{1,2},{2,3},{3,4},{4,5},{5,6},{6,7},{7,8},{8,9},{9,10},{10,1... | collective-permute-start | bytes 4616 | tf_op jit(solution)/shard_map/ppermute | solution.py:20
  52.2 7.0 %collective-permute-start.9 = (bf16[1,6,128]{2,1,0:T(8,128)(2,1)S(1)}, bf16[1,6,128]{2,1,0:T(8,128)(2,1)S(1)}, u32[]{:S(2)}, u32[]{:S(2)}) collective-permute-start(bf16[1,6,128]{2,1,0:T(8,128)(2,1)S(1)} %get-tuple-element.54), channel_id=1, source_target_pairs={{1,0},{2,1},{3,2},{4,3},{5,4},{6,5},{7,6},{8,7},{9,8},{10,9},{11,1... | collective-permute-start | bytes 4616 | tf_op jit(solution)/shard_map/ppermute | solution.py:22
  60.6 5.2 %collective-permute-start.10 = (bf16[4,1,128]{2,1,0:T(2,128)(2,1)S(1)}, bf16[4,1,128]{2,1,0:T(2,128)(2,1)S(1)}, u32[]{:S(2)}, u32[]{:S(2)}) collective-permute-start(bf16[4,1,128]{2,1,0:T(2,128)(2,1)S(1)} %get-tuple-element.55), channel_id=1, source_target_pairs={{0,32},{32,64},{64,96},{96,128},{128,160},{160,192},{192,224},{224... | collective-permute-start | bytes 3080 | tf_op jit(solution)/shard_map/ppermute | solution.py:20
  64.3 5.8 %collective-permute-start.11 = (bf16[4,1,128]{2,1,0:T(2,128)(2,1)S(1)}, bf16[4,1,128]{2,1,0:T(2,128)(2,1)S(1)}, u32[]{:S(2)}, u32[]{:S(2)}) collective-permute-start(bf16[4,1,128]{2,1,0:T(2,128)(2,1)S(1)} %get-tuple-element.56), channel_id=1, source_target_pairs={{32,0},{64,32},{96,64},{128,96},{160,128},{192,160},{224,192},{256... | collective-permute-start | bytes 3080 | tf_op jit(solution)/shard_map/ppermute | solution.py:22
  70.2 6.2 %collective-permute-start.12 = (bf16[1,6,128]{2,1,0:T(8,128)(2,1)S(1)}, bf16[1,6,128]{2,1,0:T(8,128)(2,1)S(1)}, u32[]{:S(2)}, u32[]{:S(2)}) collective-permute-start(bf16[1,6,128]{2,1,0:T(8,128)(2,1)S(1)} %get-tuple-element.49), channel_id=1, source_target_pairs={{0,1},{1,2},{2,3},{3,4},{4,5},{5,6},{6,7},{7,8},{8,9},{9,10},{10,1... | collective-permute-start | bytes 4616 | tf_op jit(solution)/shard_map/ppermute | solution.py:20
  74.2 7.0 %collective-permute-start.13 = (bf16[1,6,128]{2,1,0:T(8,128)(2,1)S(1)}, bf16[1,6,128]{2,1,0:T(8,128)(2,1)S(1)}, u32[]{:S(2)}, u32[]{:S(2)}) collective-permute-start(bf16[1,6,128]{2,1,0:T(8,128)(2,1)S(1)} %get-tuple-element.50), channel_id=1, source_target_pairs={{1,0},{2,1},{3,2},{4,3},{5,4},{6,5},{7,6},{8,7},{9,8},{10,9},{11,1... | collective-permute-start | bytes 4616 | tf_op jit(solution)/shard_map/ppermute | solution.py:22
  82.7 6.0 %collective-permute-start.14 = (bf16[8,1,128]{2,1,0:T(2,128)(2,1)S(1)}, bf16[8,1,128]{2,1,0:T(2,128)(2,1)S(1)}, u32[]{:S(2)}, u32[]{:S(2)}) collective-permute-start(bf16[8,1,128]{2,1,0:T(2,128)(2,1)S(1)} %get-tuple-element.43), channel_id=1, source_target_pairs={{0,32},{32,64},{64,96},{96,128},{128,160},{160,192},{192,224},{224... | collective-permute-start | bytes 6152 | tf_op jit(solution)/shard_map/ppermute | solution.py:20
  87.2 5.9 %collective-permute-start.15 = (bf16[8,1,128]{2,1,0:T(2,128)(2,1)S(1)}, bf16[8,1,128]{2,1,0:T(2,128)(2,1)S(1)}, u32[]{:S(2)}, u32[]{:S(2)}) collective-permute-start(bf16[8,1,128]{2,1,0:T(2,128)(2,1)S(1)} %get-tuple-element.44), channel_id=1, source_target_pairs={{32,0},{64,32},{96,64},{128,96},{160,128},{192,160},{224,192},{256... | collective-permute-start | bytes 6152 | tf_op jit(solution)/shard_map/ppermute | solution.py:22
  93.1 6.1 %collective-permute-start.16 = (bf16[1,10,128]{2,1,0:T(8,128)(2,1)S(1)}, bf16[1,10,128]{2,1,0:T(8,128)(2,1)S(1)}, u32[]{:S(2)}, u32[]{:S(2)}) collective-permute-start(bf16[1,10,128]{2,1,0:T(8,128)(2,1)S(1)} %get-tuple-element.37), channel_id=1, source_target_pairs={{0,1},{1,2},{2,3},{3,4},{4,5},{5,6},{6,7},{7,8},{8,9},{9,10},{10,1... | collective-permute-start | bytes 7688 | tf_op jit(solution)/shard_map/ppermute | solution.py:20
  97.1 7.0 %collective-permute-start.17 = (bf16[1,10,128]{2,1,0:T(8,128)(2,1)S(1)}, bf16[1,10,128]{2,1,0:T(8,128)(2,1)S(1)}, u32[]{:S(2)}, u32[]{:S(2)}) collective-permute-start(bf16[1,10,128]{2,1,0:T(8,128)(2,1)S(1)} %get-tuple-element.38), channel_id=1, source_target_pairs={{1,0},{2,1},{3,2},{4,3},{5,4},{6,5},{7,6},{8,7},{9,8},{10,9},{11,1... | collective-permute-start | bytes 7688 | tf_op jit(solution)/shard_map/ppermute | solution.py:22
  105.1 5.2 %collective-permute-start.18 = (bf16[8,1,128]{2,1,0:T(2,128)(2,1)S(1)}, bf16[8,1,128]{2,1,0:T(2,128)(2,1)S(1)}, u32[]{:S(2)}, u32[]{:S(2)}) collective-permute-start(bf16[8,1,128]{2,1,0:T(2,128)(2,1)S(1)} %get-tuple-element.41), channel_id=1, source_target_pairs={{0,32},{32,64},{64,96},{96,128},{128,160},{160,192},{192,224},{224... | collective-permute-start | bytes 6152 | tf_op jit(solution)/shard_map/ppermute | solution.py:20
  108.9 5.9 %collective-permute-start.19 = (bf16[8,1,128]{2,1,0:T(2,128)(2,1)S(1)}, bf16[8,1,128]{2,1,0:T(2,128)(2,1)S(1)}, u32[]{:S(2)}, u32[]{:S(2)}) collective-permute-start(bf16[8,1,128]{2,1,0:T(2,128)(2,1)S(1)} %get-tuple-element.42), channel_id=1, source_target_pairs={{32,0},{64,32},{96,64},{128,96},{160,128},{192,160},{224,192},{256... | collective-permute-start | bytes 6152 | tf_op jit(solution)/shard_map/ppermute | solution.py:22
  114.8 6.1 %collective-permute-start.20 = (bf16[1,10,128]{2,1,0:T(8,128)(2,1)S(1)}, bf16[1,10,128]{2,1,0:T(8,128)(2,1)S(1)}, u32[]{:S(2)}, u32[]{:S(2)}) collective-permute-start(bf16[1,10,128]{2,1,0:T(8,128)(2,1)S(1)} %get-tuple-element.33), channel_id=1, source_target_pairs={{0,1},{1,2},{2,3},{3,4},{4,5},{5,6},{6,7},{7,8},{8,9},{9,10},{10,1... | collective-permute-start | bytes 7688 | tf_op jit(solution)/shard_map/ppermute | solution.py:20
  118.8 7.0 %collective-permute-start.21 = (bf16[1,10,128]{2,1,0:T(8,128)(2,1)S(1)}, bf16[1,10,128]{2,1,0:T(8,128)(2,1)S(1)}, u32[]{:S(2)}, u32[]{:S(2)}) collective-permute-start(bf16[1,10,128]{2,1,0:T(8,128)(2,1)S(1)} %get-tuple-element.34), channel_id=1, source_target_pairs={{1,0},{2,1},{3,2},{4,3},{5,4},{6,5},{7,6},{8,7},{9,8},{10,9},{11,1... | collective-permute-start | bytes 7688 | tf_op jit(solution)/shard_map/ppermute | solution.py:22
  162.4 11.8 %collective-permute-start.22 = (bf16[20,1,128]{2,0,1:T(8,128)(2,1)S(1)}, bf16[20,1,128]{2,0,1:T(8,128)(2,1)S(1)}, u32[]{:S(2)}, u32[]{:S(2)}) collective-permute-start(bf16[20,1,128]{2,0,1:T(8,128)(2,1)S(1)} %get-tuple-element.27), channel_id=1, source_target_pairs={{0,1},{1,2},{2,3},{3,4},{4,5},{5,6},{6,7},{7,8},{8,9},{9,10},{10,1... | collective-permute-start | bytes 15368 | tf_op jit(solution)/shard_map/ppermute | solution.py:20
  172.1 7.2 %collective-permute-start.23 = (bf16[20,1,128]{2,0,1:T(8,128)(2,1)S(1)}, bf16[20,1,128]{2,0,1:T(8,128)(2,1)S(1)}, u32[]{:S(2)}, u32[]{:S(2)}) collective-permute-start(bf16[20,1,128]{2,0,1:T(8,128)(2,1)S(1)} %get-tuple-element.28), channel_id=1, source_target_pairs={{1,0},{2,1},{3,2},{4,3},{5,4},{6,5},{7,6},{8,7},{9,8},{10,9},{11,1... | collective-permute-start | bytes 15368 | tf_op jit(solution)/shard_map/ppermute | solution.py:22
  182.4 4.3 %collective-permute-start.24 = (bf16[1,128,128]{2,1,0:T(8,128)(2,1)S(1)}, bf16[1,128,128]{2,1,0:T(8,128)(2,1)S(1)}, u32[]{:S(2)}, u32[]{:S(2)}) collective-permute-start(bf16[1,128,128]{2,1,0:T(8,128)(2,1)S(1)} %get-tuple-element.15), channel_id=1, source_target_pairs={{0,1},{1,2},{2,3},{3,4},{4,5},{5,6},{6,7},{7,8},{8,9},{9,10},{10,1... | collective-permute-start | bytes 98312 | tf_op jit(solution)/shard_map/ppermute | solution.py:20
  184.4 7.3 %collective-permute-start.25 = (bf16[1,128,128]{2,1,0:T(8,128)(2,1)S(1)}, bf16[1,128,128]{2,1,0:T(8,128)(2,1)S(1)}, u32[]{:S(2)}, u32[]{:S(2)}) collective-permute-start(bf16[1,128,128]{2,1,0:T(8,128)(2,1)S(1)} %get-tuple-element.16), channel_id=1, source_target_pairs={{1,0},{2,1},{3,2},{4,3},{5,4},{6,5},{7,6},{8,7},{9,8},{10,9},{11,1... | collective-permute-start | bytes 98312 | tf_op jit(solution)/shard_map/ppermute | solution.py:22
  195.1 4.3 %collective-permute-start.26 = (bf16[1,64,128]{2,1,0:T(8,128)(2,1)S(1)}, bf16[1,64,128]{2,1,0:T(8,128)(2,1)S(1)}, u32[]{:S(2)}, u32[]{:S(2)}) collective-permute-start(bf16[1,64,128]{2,1,0:T(8,128)(2,1)S(1)} %get-tuple-element.23), channel_id=1, source_target_pairs={{0,1},{1,2},{2,3},{3,4},{4,5},{5,6},{6,7},{7,8},{8,9},{9,10},{10,1... | collective-permute-start | bytes 49160 | tf_op jit(solution)/shard_map/ppermute | solution.py:20
  197.0 7.2 %collective-permute-start.27 = (bf16[1,64,128]{2,1,0:T(8,128)(2,1)S(1)}, bf16[1,64,128]{2,1,0:T(8,128)(2,1)S(1)}, u32[]{:S(2)}, u32[]{:S(2)}) collective-permute-start(bf16[1,64,128]{2,1,0:T(8,128)(2,1)S(1)} %get-tuple-element.24), channel_id=1, source_target_pairs={{1,0},{2,1},{3,2},{4,3},{5,4},{6,5},{7,6},{8,7},{9,8},{10,9},{11,1... | collective-permute-start | bytes 49160 | tf_op jit(solution)/shard_map/ppermute | solution.py:22
  206.8 4.5 %collective-permute-start.28 = (bf16[1,64,128]{2,1,0:T(8,128)(2,1)S(1)}, bf16[1,64,128]{2,1,0:T(8,128)(2,1)S(1)}, u32[]{:S(2)}, u32[]{:S(2)}) collective-permute-start(bf16[1,64,128]{2,1,0:T(8,128)(2,1)S(1)} %get-tuple-element.21), channel_id=1, source_target_pairs={{0,1},{1,2},{2,3},{3,4},{4,5},{5,6},{6,7},{7,8},{8,9},{9,10},{10,1... | collective-permute-start | bytes 49160 | tf_op jit(solution)/shard_map/ppermute | solution.py:20
  208.8 7.2 %collective-permute-start.29 = (bf16[1,64,128]{2,1,0:T(8,128)(2,1)S(1)}, bf16[1,64,128]{2,1,0:T(8,128)(2,1)S(1)}, u32[]{:S(2)}, u32[]{:S(2)}) collective-permute-start(bf16[1,64,128]{2,1,0:T(8,128)(2,1)S(1)} %get-tuple-element.22), channel_id=1, source_target_pairs={{1,0},{2,1},{3,2},{4,3},{5,4},{6,5},{7,6},{8,7},{9,8},{10,9},{11,1... | collective-permute-start | bytes 49160 | tf_op jit(solution)/shard_map/ppermute | solution.py:22
  218.6 4.5 %collective-permute-start.30 = (bf16[1,128,128]{2,1,0:T(8,128)(2,1)S(1)}, bf16[1,128,128]{2,1,0:T(8,128)(2,1)S(1)}, u32[]{:S(2)}, u32[]{:S(2)}) collective-permute-start(bf16[1,128,128]{2,1,0:T(8,128)(2,1)S(1)} %get-tuple-element.13), channel_id=1, source_target_pairs={{0,1},{1,2},{2,3},{3,4},{4,5},{5,6},{6,7},{7,8},{8,9},{9,10},{10,1... | collective-permute-start | bytes 98312 | tf_op jit(solution)/shard_map/ppermute | solution.py:20
  220.5 7.5 %collective-permute-start.31 = (bf16[1,128,128]{2,1,0:T(8,128)(2,1)S(1)}, bf16[1,128,128]{2,1,0:T(8,128)(2,1)S(1)}, u32[]{:S(2)}, u32[]{:S(2)}) collective-permute-start(bf16[1,128,128]{2,1,0:T(8,128)(2,1)S(1)} %get-tuple-element.14), channel_id=1, source_target_pairs={{1,0},{2,1},{3,2},{4,3},{5,4},{6,5},{7,6},{8,7},{9,8},{10,9},{11,1... | collective-permute-start | bytes 98312 | tf_op jit(solution)/shard_map/ppermute | solution.py:22
  230.2 4.4 %collective-permute-start.32 = (bf16[1,128,128]{2,1,0:T(8,128)(2,1)S(1)}, bf16[1,128,128]{2,1,0:T(8,128)(2,1)S(1)}, u32[]{:S(2)}, u32[]{:S(2)}) collective-permute-start(bf16[1,128,128]{2,1,0:T(8,128)(2,1)S(1)} %get-tuple-element.11), channel_id=1, source_target_pairs={{0,1},{1,2},{2,3},{3,4},{4,5},{5,6},{6,7},{7,8},{8,9},{9,10},{10,1... | collective-permute-start | bytes 98312 | tf_op jit(solution)/shard_map/ppermute | solution.py:20
  232.1 7.3 %collective-permute-start.33 = (bf16[1,128,128]{2,1,0:T(8,128)(2,1)S(1)}, bf16[1,128,128]{2,1,0:T(8,128)(2,1)S(1)}, u32[]{:S(2)}, u32[]{:S(2)}) collective-permute-start(bf16[1,128,128]{2,1,0:T(8,128)(2,1)S(1)} %get-tuple-element.12), channel_id=1, source_target_pairs={{1,0},{2,1},{3,2},{4,3},{5,4},{6,5},{7,6},{8,7},{9,8},{10,9},{11,1... | collective-permute-start | bytes 98312 | tf_op jit(solution)/shard_map/ppermute | solution.py:22
  241.3 4.5 %collective-permute-start.34 = (bf16[20,1,128]{2,0,1:T(8,128)(2,1)S(1)}, bf16[20,1,128]{2,0,1:T(8,128)(2,1)S(1)}, u32[]{:S(2)}, u32[]{:S(2)}) collective-permute-start(bf16[20,1,128]{2,0,1:T(8,128)(2,1)S(1)} %get-tuple-element.25), channel_id=1, source_target_pairs={{0,1},{1,2},{2,3},{3,4},{4,5},{5,6},{6,7},{7,8},{8,9},{9,10},{10,1... | collective-permute-start | bytes 15368 | tf_op jit(solution)/shard_map/ppermute | solution.py:20
  243.2 7.1 %collective-permute-start.35 = (bf16[20,1,128]{2,0,1:T(8,128)(2,1)S(1)}, bf16[20,1,128]{2,0,1:T(8,128)(2,1)S(1)}, u32[]{:S(2)}, u32[]{:S(2)}) collective-permute-start(bf16[20,1,128]{2,0,1:T(8,128)(2,1)S(1)} %get-tuple-element.26), channel_id=1, source_target_pairs={{1,0},{2,1},{3,2},{4,3},{5,4},{6,5},{7,6},{8,7},{9,8},{10,9},{11,1... | collective-permute-start | bytes 15368 | tf_op jit(solution)/shard_map/ppermute | solution.py:22
  253.4 4.3 %collective-permute-start.36 = (bf16[1,128,128]{2,1,0:T(8,128)(2,1)S(1)}, bf16[1,128,128]{2,1,0:T(8,128)(2,1)S(1)}, u32[]{:S(2)}, u32[]{:S(2)}) collective-permute-start(bf16[1,128,128]{2,1,0:T(8,128)(2,1)S(1)} %get-tuple-element.9), channel_id=1, source_target_pairs={{0,1},{1,2},{2,3},{3,4},{4,5},{5,6},{6,7},{7,8},{8,9},{9,10},{10,1... | collective-permute-start | bytes 98312 | tf_op jit(solution)/shard_map/ppermute | solution.py:20
  255.3 7.3 %collective-permute-start.37 = (bf16[1,128,128]{2,1,0:T(8,128)(2,1)S(1)}, bf16[1,128,128]{2,1,0:T(8,128)(2,1)S(1)}, u32[]{:S(2)}, u32[]{:S(2)}) collective-permute-start(bf16[1,128,128]{2,1,0:T(8,128)(2,1)S(1)} %get-tuple-element.10), channel_id=1, source_target_pairs={{1,0},{2,1},{3,2},{4,3},{5,4},{6,5},{7,6},{8,7},{9,8},{10,9},{11,1... | collective-permute-start | bytes 98312 | tf_op jit(solution)/shard_map/ppermute | solution.py:22
  265.8 4.3 %collective-permute-start.38 = (bf16[1,64,128]{2,1,0:T(8,128)(2,1)S(1)}, bf16[1,64,128]{2,1,0:T(8,128)(2,1)S(1)}, u32[]{:S(2)}, u32[]{:S(2)}) collective-permute-start(bf16[1,64,128]{2,1,0:T(8,128)(2,1)S(1)} %get-tuple-element.19), channel_id=1, source_target_pairs={{0,1},{1,2},{2,3},{3,4},{4,5},{5,6},{6,7},{7,8},{8,9},{9,10},{10,1... | collective-permute-start | bytes 49160 | tf_op jit(solution)/shard_map/ppermute | solution.py:20
  267.7 7.2 %collective-permute-start.39 = (bf16[1,64,128]{2,1,0:T(8,128)(2,1)S(1)}, bf16[1,64,128]{2,1,0:T(8,128)(2,1)S(1)}, u32[]{:S(2)}, u32[]{:S(2)}) collective-permute-start(bf16[1,64,128]{2,1,0:T(8,128)(2,1)S(1)} %get-tuple-element.20), channel_id=1, source_target_pairs={{1,0},{2,1},{3,2},{4,3},{5,4},{6,5},{7,6},{8,7},{9,8},{10,9},{11,1... | collective-permute-start | bytes 49160 | tf_op jit(solution)/shard_map/ppermute | solution.py:22
  276.6 4.5 %collective-permute-start.40 = (bf16[1,64,128]{2,1,0:T(8,128)(2,1)S(1)}, bf16[1,64,128]{2,1,0:T(8,128)(2,1)S(1)}, u32[]{:S(2)}, u32[]{:S(2)}) collective-permute-start(bf16[1,64,128]{2,1,0:T(8,128)(2,1)S(1)} %get-tuple-element.17), channel_id=1, source_target_pairs={{0,1},{1,2},{2,3},{3,4},{4,5},{5,6},{6,7},{7,8},{8,9},{9,10},{10,1... | collective-permute-start | bytes 49160 | tf_op jit(solution)/shard_map/ppermute | solution.py:20
  278.6 7.2 %collective-permute-start.41 = (bf16[1,64,128]{2,1,0:T(8,128)(2,1)S(1)}, bf16[1,64,128]{2,1,0:T(8,128)(2,1)S(1)}, u32[]{:S(2)}, u32[]{:S(2)}) collective-permute-start(bf16[1,64,128]{2,1,0:T(8,128)(2,1)S(1)} %get-tuple-element.18), channel_id=1, source_target_pairs={{1,0},{2,1},{3,2},{4,3},{5,4},{6,5},{7,6},{8,7},{9,8},{10,9},{11,1... | collective-permute-start | bytes 49160 | tf_op jit(solution)/shard_map/ppermute | solution.py:22
  288.4 4.3 %collective-permute-start.42 = (bf16[1,128,128]{2,1,0:T(8,128)(2,1)S(1)}, bf16[1,128,128]{2,1,0:T(8,128)(2,1)S(1)}, u32[]{:S(2)}, u32[]{:S(2)}) collective-permute-start(bf16[1,128,128]{2,1,0:T(8,128)(2,1)S(1)} %get-tuple-element.7), channel_id=1, source_target_pairs={{0,1},{1,2},{2,3},{3,4},{4,5},{5,6},{6,7},{7,8},{8,9},{9,10},{10,1... | collective-permute-start | bytes 98312 | tf_op jit(solution)/shard_map/ppermute | solution.py:20
  290.3 7.3 %collective-permute-start.43 = (bf16[1,128,128]{2,1,0:T(8,128)(2,1)S(1)}, bf16[1,128,128]{2,1,0:T(8,128)(2,1)S(1)}, u32[]{:S(2)}, u32[]{:S(2)}) collective-permute-start(bf16[1,128,128]{2,1,0:T(8,128)(2,1)S(1)} %get-tuple-element.8), channel_id=1, source_target_pairs={{1,0},{2,1},{3,2},{4,3},{5,4},{6,5},{7,6},{8,7},{9,8},{10,9},{11,1... | collective-permute-start | bytes 98312 | tf_op jit(solution)/shard_map/ppermute | solution.py:22
  299.8 4.3 %collective-permute-start.44 = (bf16[1,128,128]{2,1,0:T(8,128)(2,1)S(1)}, bf16[1,128,128]{2,1,0:T(8,128)(2,1)S(1)}, u32[]{:S(2)}, u32[]{:S(2)}) collective-permute-start(bf16[1,128,128]{2,1,0:T(8,128)(2,1)S(1)} %get-tuple-element.5), channel_id=1, source_target_pairs={{0,1},{1,2},{2,3},{3,4},{4,5},{5,6},{6,7},{7,8},{8,9},{9,10},{10,1... | collective-permute-start | bytes 98312 | tf_op jit(solution)/shard_map/ppermute | solution.py:20
  301.8 7.3 %collective-permute-start.45 = (bf16[1,128,128]{2,1,0:T(8,128)(2,1)S(1)}, bf16[1,128,128]{2,1,0:T(8,128)(2,1)S(1)}, u32[]{:S(2)}, u32[]{:S(2)}) collective-permute-start(bf16[1,128,128]{2,1,0:T(8,128)(2,1)S(1)} %get-tuple-element.6), channel_id=1, source_target_pairs={{1,0},{2,1},{3,2},{4,3},{5,4},{6,5},{7,6},{8,7},{9,8},{10,9},{11,1... | collective-permute-start | bytes 98312 | tf_op jit(solution)/shard_map/ppermute | solution.py:22
  (12 other events, 62.7 us)
where the time goes:
time: 313 us; the launch traced here: 312 us
  starting transfers between devices  128 us (41%)
  waiting for transfers between devices  105 us (34%)
  blocking collectives  35 us (11%)
  matrix products  31.9 us (10%)
  local copies, waits for them, and re-layouts  8.36 us (3%)
    ppermute x23, waiting for transfers between devices, with_halo(): lax.ppermute(head, axis, [((i + 1) % count, i) for i in range(ends)])  104 us
    ppermute x23, starting transfers between devices, with_halo(): lax.ppermute(tail, axis, [(i, (i + 1) % count) for i in range(ends)])  80.6 us
    ppermute x23, starting transfers between devices, with_halo(): lax.ppermute(head, axis, [((i + 1) % count, i) for i in range(ends)])  47.4 us
    all_gather x1, blocking collectives, shards(): reg_mean = lax.all_gather(mean_strip, 'ens', axis=2, tiled=True)  35 us
    dot_general x81, matrix products, conv_feat(): jnp.dot(window, weight[tap_y, tap_x], preferred_element_type=jnp.float32)  13 us
    dot_general x27, matrix products, conv_fields(): jnp.einsum('crw,co->rwo', window, weight[tap_y, tap_x], preferred_element...  7.14 us
    dot_general x48, matrix products, parity(): jnp.dot(window, weight[kernel_y, kernel_x], preferred_element_type=jnp.fl...  6.79 us
  transfers between devices with their start and end apart: 46, of which 23 were waited for; matrix products, arithmetic and copies ran while one was open for 1% of the time, Pallas kernels for 0%

commit v1 on v0

--- a/solution.py
+++ b/solution.py
@@ -1,12 +1,24 @@
+import functools
 import jax
 import jax.numpy as jnp
 from jax import lax
 from jax.sharding import PartitionSpec as P
+from jax.lax import all_to_all, psum
 
 STEPS = 2
 sigma_top = 1.0
 sigma_ratio = 0.4
 sigma_data = 0.5
+
+
+def bind_local_data_by_axis(m, net_axis):
+    aux = psum(1, net_axis)
+    d_next = jnp.stack([m] * aux, axis=0)
+    out_arr = all_to_all(d_next, net_axis, 0, 0)
+    return jnp.concatenate(out_arr, 2)
+
+
+choose_cube = functools.partial(bind_local_data_by_axis, net_axis="ens")
 
 
 def with_halo(cells, sides, width):
@@ -147,7 +159,7 @@
     strip_start = lax.axis_index("ens") * strip_width
     strip_input = lax.dynamic_slice_in_dim(cond_padded, strip_start, strip_width + 2, 2)
     mean_strip = network_pass(strip_input, reg_weights, strip_pad, lower_each)
-    reg_mean = lax.all_gather(mean_strip, "ens", axis=2, tiled=True)
+    reg_mean = choose_cube(mean_strip)
     mean_input = reg_mean.astype(jnp.bfloat16)
     residual_field = sigma_top * member_noise[0]
     for step_index in range(STEPS):

time: 313 us -> 294 us (0.939)
  blocking collectives: 35 us -> 0 us
  waiting for transfers between devices: 105 us -> 114 us
  starting transfers between devices: 128 us -> 133 us
    all_gather x1 -> x0, blocking collectives: 35 us -> none  [shards(): reg_mean = lax.all_gather(mean_strip, 'ens', axis=2, tiled=True)]
    all_to_all x0 -> x1, starting transfers between devices: none -> 10.2 us  [bind_local_data_by_axis(): out_arr = all_to_all(d_next, net_axis, 0, 0)]
    all_to_all x0 -> x1, waiting for transfers between devices: none -> 8.88 us  [bind_local_data_by_axis(): out_arr = all_to_all(d_next, net_axis, 0, 0)]
    ppermute x23, starting transfers between devices: 80.6 us -> 74.9 us  [with_halo(): lax.ppermute(tail, axis, [(i, (i + 1) % count) for i in range(ends)])]
  transfers between devices with their start and end apart: 46 -> 47, of which waited for: 23 -> 24; matrix products, arithmetic and copies ran while one was open for 1% -> 1% of each run, Pallas kernels for 0% -> 0%
where the time goes in v1:
time: 294 us; the launch traced here: 292 us
  starting transfers between devices  133 us (45%)
  waiting for transfers between devices  114 us (39%)
  matrix products  31.9 us (11%)
  local copies, waits for them, and re-layouts  9.97 us (3%)
    ppermute x23, waiting for transfers between devices, with_halo(): lax.ppermute(head, axis, [((i + 1) % count, i) for i in range(ends)])  104 us
    ppermute x23, starting transfers between devices, with_halo(): lax.ppermute(tail, axis, [(i, (i + 1) % count) for i in range(ends)])  74.9 us
    ppermute x23, starting transfers between devices, with_halo(): lax.ppermute(head, axis, [((i + 1) % count, i) for i in range(ends)])  47.5 us
    dot_general x81, matrix products, conv_feat(): jnp.dot(window, weight[tap_y, tap_x], preferred_element_type=jnp.float32)  13 us
    all_to_all x1, starting transfers between devices, bind_local_data_by_axis(): out_arr = all_to_all(d_next, net_axis, 0, 0)  10.2 us
    all_to_all x1, waiting for transfers between devices, bind_local_data_by_axis(): out_arr = all_to_all(d_next, net_axis, 0, 0)  8.88 us
    dot_general x27, matrix products, conv_fields(): jnp.einsum('crw,co->rwo', window, weight[tap_y, tap_x], preferred_element...  7.13 us
    dot_general x48, matrix products, parity(): jnp.dot(window, weight[kernel_y, kernel_x], preferred_element_type=jnp.fl...  6.79 us
  transfers between devices with their start and end apart: 47, of which 24 were waited for; matrix products, arithmetic and copies ran while one was open for 1% of the time, Pallas kernels for 0%

profile of v1, /device:TPU:27, one launch (start us, length us, event | category | flops | bytes accessed | tf_op | source)
XLA Modules:
  0.0 292.3 jit_solution(14985445322803164407)
XLA Ops:
  1.0 2.7 collective-permute-start.1
  3.8 5.1 %collective-permute-start = (bf16[12,1,128]{0,2,1:T(8,128)(2,1)S(1)}, bf16[12,1,128]{0,2,1:T(8,128)(2,1)S(1)}, u32[]{:S(2)}, u32[]{:S(2)}) collective-permute-start(bf16[12,1,128]{0,2,1:T(8,128)(2,1)S(1)} %copy.53), channel_id=1, source_target_pairs={{0,1},{1,2},{2,3},{3,4},{4,5},{5,6},{6,7},{7,8},{8,9},{9,10},{10,1... | collective-permute-start | bytes 9224 | tf_op jit(solution)/shard_map/ppermute | solution.py:32
  11.5 3.7 %collective-permute-start.2 = (bf16[8,1,128]{2,1,0:T(2,128)(2,1)S(1)}, bf16[8,1,128]{2,1,0:T(2,128)(2,1)S(1)}, u32[]{:S(2)}, u32[]{:S(2)}) collective-permute-start(bf16[8,1,128]{2,1,0:T(2,128)(2,1)S(1)} %get-tuple-element.45), channel_id=1, source_target_pairs={{0,32},{32,64},{64,96},{96,128},{128,160},{160,192},{192,224},{224... | collective-permute-start | bytes 6152 | tf_op jit(solution)/shard_map/ppermute | solution.py:32
  17.1 4.0 %collective-permute-done.3 = bf16[8,1,128]{2,1,0:T(2,128)(2,1)S(1)} collective-permute-done((bf16[8,1,128]{2,1,0:T(2,128)(2,1)S(1)}, bf16[8,1,128]{2,1,0:T(2,128)(2,1)S(1)}, u32[]{:S(2)}, u32[]{:S(2)}) %collective-permute-start.3) | collective-permute-done | bytes 2080 | tf_op jit(solution)/shard_map/ppermute | solution.py:34
  21.2 8.4 %collective-permute-start.4 = (bf16[1,10,128]{2,1,0:T(8,128)(2,1)S(1)}, bf16[1,10,128]{2,1,0:T(8,128)(2,1)S(1)}, u32[]{:S(2)}, u32[]{:S(2)}) collective-permute-start(bf16[1,10,128]{2,1,0:T(8,128)(2,1)S(1)} %get-tuple-element.29), channel_id=1, source_target_pairs={{0,1},{1,2},{2,3},{3,4},{4,5},{5,6},{6,7},{7,8},{8,9},{9,10},{10,1... | collective-permute-start | bytes 7688 | tf_op jit(solution)/shard_map/ppermute | solution.py:32
  31.8 4.8 %collective-permute-done.5 = bf16[1,10,128]{2,1,0:T(8,128)(2,1)S(1)} collective-permute-done((bf16[1,10,128]{2,1,0:T(8,128)(2,1)S(1)}, bf16[1,10,128]{2,1,0:T(8,128)(2,1)S(1)}, u32[]{:S(2)}, u32[]{:S(2)}) %collective-permute-start.5) | collective-permute-done | bytes 2592 | tf_op jit(solution)/shard_map/ppermute | solution.py:34
  37.9 4.5 %collective-permute-start.6 = (bf16[4,1,128]{2,1,0:T(2,128)(2,1)S(1)}, bf16[4,1,128]{2,1,0:T(2,128)(2,1)S(1)}, u32[]{:S(2)}, u32[]{:S(2)}) collective-permute-start(bf16[4,1,128]{2,1,0:T(2,128)(2,1)S(1)} %get-tuple-element.57), channel_id=1, source_target_pairs={{0,32},{32,64},{64,96},{96,128},{128,160},{160,192},{192,224},{224... | collective-permute-start | bytes 3080 | tf_op jit(solution)/shard_map/ppermute | solution.py:32
  43.9 4.4 %collective-permute-done.7 = bf16[4,1,128]{2,1,0:T(2,128)(2,1)S(1)} collective-permute-done((bf16[4,1,128]{2,1,0:T(2,128)(2,1)S(1)}, bf16[4,1,128]{2,1,0:T(2,128)(2,1)S(1)}, u32[]{:S(2)}, u32[]{:S(2)}) %collective-permute-start.7) | collective-permute-done | bytes 1056 | tf_op jit(solution)/shard_map/ppermute | solution.py:34
  48.3 4.0 %collective-permute-start.8 = (bf16[1,6,128]{2,1,0:T(8,128)(2,1)S(1)}, bf16[1,6,128]{2,1,0:T(8,128)(2,1)S(1)}, u32[]{:S(2)}, u32[]{:S(2)}) collective-permute-start(bf16[1,6,128]{2,1,0:T(8,128)(2,1)S(1)} %get-tuple-element.53), channel_id=1, source_target_pairs={{0,1},{1,2},{2,3},{3,4},{4,5},{5,6},{6,7},{7,8},{8,9},{9,10},{10,1... | collective-permute-start | bytes 4616 | tf_op jit(solution)/shard_map/ppermute | solution.py:32
  54.3 4.9 %collective-permute-done.9 = bf16[1,6,128]{2,1,0:T(8,128)(2,1)S(1)} collective-permute-done((bf16[1,6,128]{2,1,0:T(8,128)(2,1)S(1)}, bf16[1,6,128]{2,1,0:T(8,128)(2,1)S(1)}, u32[]{:S(2)}, u32[]{:S(2)}) %collective-permute-start.9) | collective-permute-done | bytes 1568 | tf_op jit(solution)/shard_map/ppermute | solution.py:34
  60.7 3.8 %collective-permute-start.10 = (bf16[4,1,128]{2,1,0:T(2,128)(2,1)S(1)}, bf16[4,1,128]{2,1,0:T(2,128)(2,1)S(1)}, u32[]{:S(2)}, u32[]{:S(2)}) collective-permute-start(bf16[4,1,128]{2,1,0:T(2,128)(2,1)S(1)} %get-tuple-element.55), channel_id=1, source_target_pairs={{0,32},{32,64},{64,96},{96,128},{128,160},{160,192},{192,224},{224... | collective-permute-start | bytes 3080 | tf_op jit(solution)/shard_map/ppermute | solution.py:32
  65.9 4.4 %collective-permute-done.11 = bf16[4,1,128]{2,1,0:T(2,128)(2,1)S(1)} collective-permute-done((bf16[4,1,128]{2,1,0:T(2,128)(2,1)S(1)}, bf16[4,1,128]{2,1,0:T(2,128)(2,1)S(1)}, u32[]{:S(2)}, u32[]{:S(2)}) %collective-permute-start.11) | collective-permute-done | bytes 1056 | tf_op jit(solution)/shard_map/ppermute | solution.py:34
  70.3 4.0 %collective-permute-start.12 = (bf16[1,6,128]{2,1,0:T(8,128)(2,1)S(1)}, bf16[1,6,128]{2,1,0:T(8,128)(2,1)S(1)}, u32[]{:S(2)}, u32[]{:S(2)}) collective-permute-start(bf16[1,6,128]{2,1,0:T(8,128)(2,1)S(1)} %get-tuple-element.49), channel_id=1, source_target_pairs={{0,1},{1,2},{2,3},{3,4},{4,5},{5,6},{6,7},{7,8},{8,9},{9,10},{10,1... | collective-permute-start | bytes 4616 | tf_op jit(solution)/shard_map/ppermute | solution.py:32
  76.5 4.8 %collective-permute-done.13 = bf16[1,6,128]{2,1,0:T(8,128)(2,1)S(1)} collective-permute-done((bf16[1,6,128]{2,1,0:T(8,128)(2,1)S(1)}, bf16[1,6,128]{2,1,0:T(8,128)(2,1)S(1)}, u32[]{:S(2)}, u32[]{:S(2)}) %collective-permute-start.13) | collective-permute-done | bytes 1568 | tf_op jit(solution)/shard_map/ppermute | solution.py:34
  82.8 4.5 %collective-permute-start.14 = (bf16[8,1,128]{2,1,0:T(2,128)(2,1)S(1)}, bf16[8,1,128]{2,1,0:T(2,128)(2,1)S(1)}, u32[]{:S(2)}, u32[]{:S(2)}) collective-permute-start(bf16[8,1,128]{2,1,0:T(2,128)(2,1)S(1)} %get-tuple-element.43), channel_id=1, source_target_pairs={{0,32},{32,64},{64,96},{96,128},{128,160},{160,192},{192,224},{224... | collective-permute-start | bytes 6152 | tf_op jit(solution)/shard_map/ppermute | solution.py:32
  88.8 4.4 %collective-permute-done.15 = bf16[8,1,128]{2,1,0:T(2,128)(2,1)S(1)} collective-permute-done((bf16[8,1,128]{2,1,0:T(2,128)(2,1)S(1)}, bf16[8,1,128]{2,1,0:T(2,128)(2,1)S(1)}, u32[]{:S(2)}, u32[]{:S(2)}) %collective-permute-start.15) | collective-permute-done | bytes 2080 | tf_op jit(solution)/shard_map/ppermute | solution.py:34
  93.2 4.0 %collective-permute-start.16 = (bf16[1,10,128]{2,1,0:T(8,128)(2,1)S(1)}, bf16[1,10,128]{2,1,0:T(8,128)(2,1)S(1)}, u32[]{:S(2)}, u32[]{:S(2)}) collective-permute-start(bf16[1,10,128]{2,1,0:T(8,128)(2,1)S(1)} %get-tuple-element.37), channel_id=1, source_target_pairs={{0,1},{1,2},{2,3},{3,4},{4,5},{5,6},{6,7},{7,8},{8,9},{9,10},{10,1... | collective-permute-start | bytes 7688 | tf_op jit(solution)/shard_map/ppermute | solution.py:32
  99.2 5.0 %collective-permute-done.17 = bf16[1,10,128]{2,1,0:T(8,128)(2,1)S(1)} collective-permute-done((bf16[1,10,128]{2,1,0:T(8,128)(2,1)S(1)}, bf16[1,10,128]{2,1,0:T(8,128)(2,1)S(1)}, u32[]{:S(2)}, u32[]{:S(2)}) %collective-permute-start.17) | collective-permute-done | bytes 2592 | tf_op jit(solution)/shard_map/ppermute | solution.py:34
  105.2 3.8 %collective-permute-start.18 = (bf16[8,1,128]{2,1,0:T(2,128)(2,1)S(1)}, bf16[8,1,128]{2,1,0:T(2,128)(2,1)S(1)}, u32[]{:S(2)}, u32[]{:S(2)}) collective-permute-start(bf16[8,1,128]{2,1,0:T(2,128)(2,1)S(1)} %get-tuple-element.41), channel_id=1, source_target_pairs={{0,32},{32,64},{64,96},{96,128},{128,160},{160,192},{192,224},{224... | collective-permute-start | bytes 6152 | tf_op jit(solution)/shard_map/ppermute | solution.py:32
  110.5 4.4 %collective-permute-done.19 = bf16[8,1,128]{2,1,0:T(2,128)(2,1)S(1)} collective-permute-done((bf16[8,1,128]{2,1,0:T(2,128)(2,1)S(1)}, bf16[8,1,128]{2,1,0:T(2,128)(2,1)S(1)}, u32[]{:S(2)}, u32[]{:S(2)}) %collective-permute-start.19) | collective-permute-done | bytes 2080 | tf_op jit(solution)/shard_map/ppermute | solution.py:34
  114.9 4.0 %collective-permute-start.20 = (bf16[1,10,128]{2,1,0:T(8,128)(2,1)S(1)}, bf16[1,10,128]{2,1,0:T(8,128)(2,1)S(1)}, u32[]{:S(2)}, u32[]{:S(2)}) collective-permute-start(bf16[1,10,128]{2,1,0:T(8,128)(2,1)S(1)} %get-tuple-element.33), channel_id=1, source_target_pairs={{0,1},{1,2},{2,3},{3,4},{4,5},{5,6},{6,7},{7,8},{8,9},{9,10},{10,1... | collective-permute-start | bytes 7688 | tf_op jit(solution)/shard_map/ppermute | solution.py:32
  121.0 4.9 %collective-permute-done.21 = bf16[1,10,128]{2,1,0:T(8,128)(2,1)S(1)} collective-permute-done((bf16[1,10,128]{2,1,0:T(8,128)(2,1)S(1)}, bf16[1,10,128]{2,1,0:T(8,128)(2,1)S(1)}, u32[]{:S(2)}, u32[]{:S(2)}) %collective-permute-start.21) | collective-permute-done | bytes 2592 | tf_op jit(solution)/shard_map/ppermute | solution.py:34
  128.1 10.2 %all-to-all-start = ((f32[16,1,256]{2,1,0:T(1,128)}), f32[16,1,256]{2,1,0:T(1,128)S(1)}, u32[]{:S(2)}, u32[]{:S(2)}) async-start(f32[16,1,256]{2,1,0:T(1,128)} %reshape.145), calls=%async_computation | async-start | bytes 32768 | tf_op jit(solution)/shard_map/all_to_all | solution.py:17
  138.3 8.9 %all-to-all-done = f32[16,1,256]{2,1,0:T(1,128)S(1)} async-done(((f32[16,1,256]{2,1,0:T(1,128)}), f32[16,1,256]{2,1,0:T(1,128)S(1)}, u32[]{:S(2)}, u32[]{:S(2)}) %all-to-all-start) | async-done | bytes 16416 | tf_op jit(solution)/shard_map/all_to_all | solution.py:17
  149.0 4.0 %collective-permute-start.22 = (bf16[20,1,128]{2,0,1:T(8,128)(2,1)S(1)}, bf16[20,1,128]{2,0,1:T(8,128)(2,1)S(1)}, u32[]{:S(2)}, u32[]{:S(2)}) collective-permute-start(bf16[20,1,128]{2,0,1:T(8,128)(2,1)S(1)} %get-tuple-element.27), channel_id=1, source_target_pairs={{0,1},{1,2},{2,3},{3,4},{4,5},{5,6},{6,7},{7,8},{8,9},{9,10},{10,1... | collective-permute-start | bytes 15368 | tf_op jit(solution)/shard_map/ppermute | solution.py:32
  155.0 5.1 %collective-permute-done.23 = bf16[20,1,128]{2,0,1:T(8,128)(2,1)S(1)} collective-permute-done((bf16[20,1,128]{2,0,1:T(8,128)(2,1)S(1)}, bf16[20,1,128]{2,0,1:T(8,128)(2,1)S(1)}, u32[]{:S(2)}, u32[]{:S(2)}) %collective-permute-start.23) | collective-permute-done | bytes 5152 | tf_op jit(solution)/shard_map/ppermute | solution.py:34
  165.2 2.4 collective-permute-start.25
  167.6 4.9 %collective-permute-done.25 = bf16[1,128,128]{2,1,0:T(8,128)(2,1)S(1)} collective-permute-done((bf16[1,128,128]{2,1,0:T(8,128)(2,1)S(1)}, bf16[1,128,128]{2,1,0:T(8,128)(2,1)S(1)}, u32[]{:S(2)}, u32[]{:S(2)}) %collective-permute-start.25) | collective-permute-done | bytes 32800 | tf_op jit(solution)/shard_map/ppermute | solution.py:34
  177.9 2.4 collective-permute-start.27
  180.3 4.7 %collective-permute-done.27 = bf16[1,64,128]{2,1,0:T(8,128)(2,1)S(1)} collective-permute-done((bf16[1,64,128]{2,1,0:T(8,128)(2,1)S(1)}, bf16[1,64,128]{2,1,0:T(8,128)(2,1)S(1)}, u32[]{:S(2)}, u32[]{:S(2)}) %collective-permute-start.27) | collective-permute-done | bytes 16416 | tf_op jit(solution)/shard_map/ppermute | solution.py:34
  189.6 2.4 collective-permute-start.29
  192.1 4.6 %collective-permute-done.29 = bf16[1,64,128]{2,1,0:T(8,128)(2,1)S(1)} collective-permute-done((bf16[1,64,128]{2,1,0:T(8,128)(2,1)S(1)}, bf16[1,64,128]{2,1,0:T(8,128)(2,1)S(1)}, u32[]{:S(2)}, u32[]{:S(2)}) %collective-permute-start.29) | collective-permute-done | bytes 16416 | tf_op jit(solution)/shard_map/ppermute | solution.py:34
  201.3 2.5 collective-permute-start.31
  203.9 4.9 %collective-permute-done.31 = bf16[1,128,128]{2,1,0:T(8,128)(2,1)S(1)} collective-permute-done((bf16[1,128,128]{2,1,0:T(8,128)(2,1)S(1)}, bf16[1,128,128]{2,1,0:T(8,128)(2,1)S(1)}, u32[]{:S(2)}, u32[]{:S(2)}) %collective-permute-start.31) | collective-permute-done | bytes 32800 | tf_op jit(solution)/shard_map/ppermute | solution.py:34
  212.9 2.4 collective-permute-start.33
  215.4 4.9 %collective-permute-done.33 = bf16[1,128,128]{2,1,0:T(8,128)(2,1)S(1)} collective-permute-done((bf16[1,128,128]{2,1,0:T(8,128)(2,1)S(1)}, bf16[1,128,128]{2,1,0:T(8,128)(2,1)S(1)}, u32[]{:S(2)}, u32[]{:S(2)}) %collective-permute-start.33) | collective-permute-done | bytes 32800 | tf_op jit(solution)/shard_map/ppermute | solution.py:34
  224.1 2.6 collective-permute-start.35
  226.7 4.5 %collective-permute-done.35 = bf16[20,1,128]{2,0,1:T(8,128)(2,1)S(1)} collective-permute-done((bf16[20,1,128]{2,0,1:T(8,128)(2,1)S(1)}, bf16[20,1,128]{2,0,1:T(8,128)(2,1)S(1)}, u32[]{:S(2)}, u32[]{:S(2)}) %collective-permute-start.35) | collective-permute-done | bytes 5152 | tf_op jit(solution)/shard_map/ppermute | solution.py:34
  236.2 2.4 collective-permute-start.37
  238.6 4.9 %collective-permute-done.37 = bf16[1,128,128]{2,1,0:T(8,128)(2,1)S(1)} collective-permute-done((bf16[1,128,128]{2,1,0:T(8,128)(2,1)S(1)}, bf16[1,128,128]{2,1,0:T(8,128)(2,1)S(1)}, u32[]{:S(2)}, u32[]{:S(2)}) %collective-permute-start.37) | collective-permute-done | bytes 32800 | tf_op jit(solution)/shard_map/ppermute | solution.py:34
  248.5 2.4 collective-permute-start.39
  251.0 4.7 %collective-permute-done.39 = bf16[1,64,128]{2,1,0:T(8,128)(2,1)S(1)} collective-permute-done((bf16[1,64,128]{2,1,0:T(8,128)(2,1)S(1)}, bf16[1,64,128]{2,1,0:T(8,128)(2,1)S(1)}, u32[]{:S(2)}, u32[]{:S(2)}) %collective-permute-start.39) | collective-permute-done | bytes 16416 | tf_op jit(solution)/shard_map/ppermute | solution.py:34
  259.4 2.4 collective-permute-start.41
  262.0 4.6 %collective-permute-done.41 = bf16[1,64,128]{2,1,0:T(8,128)(2,1)S(1)} collective-permute-done((bf16[1,64,128]{2,1,0:T(8,128)(2,1)S(1)}, bf16[1,64,128]{2,1,0:T(8,128)(2,1)S(1)}, u32[]{:S(2)}, u32[]{:S(2)}) %collective-permute-start.41) | collective-permute-done | bytes 16416 | tf_op jit(solution)/shard_map/ppermute | solution.py:34
  271.1 2.4 collective-permute-start.43
  273.5 4.9 %collective-permute-done.43 = bf16[1,128,128]{2,1,0:T(8,128)(2,1)S(1)} collective-permute-done((bf16[1,128,128]{2,1,0:T(8,128)(2,1)S(1)}, bf16[1,128,128]{2,1,0:T(8,128)(2,1)S(1)}, u32[]{:S(2)}, u32[]{:S(2)}) %collective-permute-start.43) | collective-permute-done | bytes 32800 | tf_op jit(solution)/shard_map/ppermute | solution.py:34
  282.6 2.4 collective-permute-start.45
  285.0 4.9 %collective-permute-done.45 = bf16[1,128,128]{2,1,0:T(8,128)(2,1)S(1)} collective-permute-done((bf16[1,128,128]{2,1,0:T(8,128)(2,1)S(1)}, bf16[1,128,128]{2,1,0:T(8,128)(2,1)S(1)}, u32[]{:S(2)}, u32[]{:S(2)}) %collective-permute-start.45) | collective-permute-done | bytes 32800 | tf_op jit(solution)/shard_map/ppermute | solution.py:34
  (357 shorter events, 84.3 us)
Async XLA Ops:
  1.0 8.2 %collective-permute-start.1 = (bf16[12,1,128]{0,2,1:T(8,128)(2,1)S(1)}, bf16[12,1,128]{0,2,1:T(8,128)(2,1)S(1)}, u32[]{:S(2)}, u32[]{:S(2)}) collective-permute-start(bf16[12,1,128]{0,2,1:T(8,128)(2,1)S(1)} %copy.54), channel_id=1, source_target_pairs={{1,0},{2,1},{3,2},{4,3},{5,4},{6,5},{7,6},{8,7},{9,8},{10,9},{11,1... | collective-permute-start | bytes 9224 | tf_op jit(solution)/shard_map/ppermute | solution.py:34
  3.8 6.1 %collective-permute-start = (bf16[12,1,128]{0,2,1:T(8,128)(2,1)S(1)}, bf16[12,1,128]{0,2,1:T(8,128)(2,1)S(1)}, u32[]{:S(2)}, u32[]{:S(2)}) collective-permute-start(bf16[12,1,128]{0,2,1:T(8,128)(2,1)S(1)} %copy.53), channel_id=1, source_target_pairs={{0,1},{1,2},{2,3},{3,4},{4,5},{5,6},{6,7},{7,8},{8,9},{9,10},{10,1... | collective-permute-start | bytes 9224 | tf_op jit(solution)/shard_map/ppermute | solution.py:32
  11.5 5.6 %collective-permute-start.2 = (bf16[8,1,128]{2,1,0:T(2,128)(2,1)S(1)}, bf16[8,1,128]{2,1,0:T(2,128)(2,1)S(1)}, u32[]{:S(2)}, u32[]{:S(2)}) collective-permute-start(bf16[8,1,128]{2,1,0:T(2,128)(2,1)S(1)} %get-tuple-element.45), channel_id=1, source_target_pairs={{0,32},{32,64},{64,96},{96,128},{128,160},{160,192},{192,224},{224... | collective-permute-start | bytes 6152 | tf_op jit(solution)/shard_map/ppermute | solution.py:32
  15.2 5.9 %collective-permute-start.3 = (bf16[8,1,128]{2,1,0:T(2,128)(2,1)S(1)}, bf16[8,1,128]{2,1,0:T(2,128)(2,1)S(1)}, u32[]{:S(2)}, u32[]{:S(2)}) collective-permute-start(bf16[8,1,128]{2,1,0:T(2,128)(2,1)S(1)} %get-tuple-element.46), channel_id=1, source_target_pairs={{32,0},{64,32},{96,64},{128,96},{160,128},{192,160},{224,192},{256... | collective-permute-start | bytes 6152 | tf_op jit(solution)/shard_map/ppermute | solution.py:34
  21.2 10.6 %collective-permute-start.4 = (bf16[1,10,128]{2,1,0:T(8,128)(2,1)S(1)}, bf16[1,10,128]{2,1,0:T(8,128)(2,1)S(1)}, u32[]{:S(2)}, u32[]{:S(2)}) collective-permute-start(bf16[1,10,128]{2,1,0:T(8,128)(2,1)S(1)} %get-tuple-element.29), channel_id=1, source_target_pairs={{0,1},{1,2},{2,3},{3,4},{4,5},{5,6},{6,7},{7,8},{8,9},{9,10},{10,1... | collective-permute-start | bytes 7688 | tf_op jit(solution)/shard_map/ppermute | solution.py:32
  29.6 7.0 %collective-permute-start.5 = (bf16[1,10,128]{2,1,0:T(8,128)(2,1)S(1)}, bf16[1,10,128]{2,1,0:T(8,128)(2,1)S(1)}, u32[]{:S(2)}, u32[]{:S(2)}) collective-permute-start(bf16[1,10,128]{2,1,0:T(8,128)(2,1)S(1)} %get-tuple-element.30), channel_id=1, source_target_pairs={{1,0},{2,1},{3,2},{4,3},{5,4},{6,5},{7,6},{8,7},{9,8},{10,9},{11,1... | collective-permute-start | bytes 7688 | tf_op jit(solution)/shard_map/ppermute | solution.py:34
  36.7 23.6 %copy-start.4 = (bf16[4,4,128,128]{3,2,1,0:T(8,128)(2,1)S(1)}, bf16[4,4,128,128]{3,2,1,0:T(8,128)(2,1)}, u32[]{:S(2)}) copy-start(bf16[4,4,128,128]{3,2,1,0:T(8,128)(2,1)} %param.19) | copy-start | bytes 1572868
  37.9 6.0 %collective-permute-start.6 = (bf16[4,1,128]{2,1,0:T(2,128)(2,1)S(1)}, bf16[4,1,128]{2,1,0:T(2,128)(2,1)S(1)}, u32[]{:S(2)}, u32[]{:S(2)}) collective-permute-start(bf16[4,1,128]{2,1,0:T(2,128)(2,1)S(1)} %get-tuple-element.57), channel_id=1, source_target_pairs={{0,32},{32,64},{64,96},{96,128},{128,160},{160,192},{192,224},{224... | collective-permute-start | bytes 3080 | tf_op jit(solution)/shard_map/ppermute | solution.py:32
  42.4 5.8 %collective-permute-start.7 = (bf16[4,1,128]{2,1,0:T(2,128)(2,1)S(1)}, bf16[4,1,128]{2,1,0:T(2,128)(2,1)S(1)}, u32[]{:S(2)}, u32[]{:S(2)}) collective-permute-start(bf16[4,1,128]{2,1,0:T(2,128)(2,1)S(1)} %get-tuple-element.58), channel_id=1, source_target_pairs={{32,0},{64,32},{96,64},{128,96},{160,128},{192,160},{224,192},{256... | collective-permute-start | bytes 3080 | tf_op jit(solution)/shard_map/ppermute | solution.py:34
  48.3 6.1 %collective-permute-start.8 = (bf16[1,6,128]{2,1,0:T(8,128)(2,1)S(1)}, bf16[1,6,128]{2,1,0:T(8,128)(2,1)S(1)}, u32[]{:S(2)}, u32[]{:S(2)}) collective-permute-start(bf16[1,6,128]{2,1,0:T(8,128)(2,1)S(1)} %get-tuple-element.53), channel_id=1, source_target_pairs={{0,1},{1,2},{2,3},{3,4},{4,5},{5,6},{6,7},{7,8},{8,9},{9,10},{10,1... | collective-permute-start | bytes 4616 | tf_op jit(solution)/shard_map/ppermute | solution.py:32
  52.3 7.0 %collective-permute-start.9 = (bf16[1,6,128]{2,1,0:T(8,128)(2,1)S(1)}, bf16[1,6,128]{2,1,0:T(8,128)(2,1)S(1)}, u32[]{:S(2)}, u32[]{:S(2)}) collective-permute-start(bf16[1,6,128]{2,1,0:T(8,128)(2,1)S(1)} %get-tuple-element.54), channel_id=1, source_target_pairs={{1,0},{2,1},{3,2},{4,3},{5,4},{6,5},{7,6},{8,7},{9,8},{10,9},{11,1... | collective-permute-start | bytes 4616 | tf_op jit(solution)/shard_map/ppermute | solution.py:34
  60.7 5.2 %collective-permute-start.10 = (bf16[4,1,128]{2,1,0:T(2,128)(2,1)S(1)}, bf16[4,1,128]{2,1,0:T(2,128)(2,1)S(1)}, u32[]{:S(2)}, u32[]{:S(2)}) collective-permute-start(bf16[4,1,128]{2,1,0:T(2,128)(2,1)S(1)} %get-tuple-element.55), channel_id=1, source_target_pairs={{0,32},{32,64},{64,96},{96,128},{128,160},{160,192},{192,224},{224... | collective-permute-start | bytes 3080 | tf_op jit(solution)/shard_map/ppermute | solution.py:32
  64.4 5.8 %collective-permute-start.11 = (bf16[4,1,128]{2,1,0:T(2,128)(2,1)S(1)}, bf16[4,1,128]{2,1,0:T(2,128)(2,1)S(1)}, u32[]{:S(2)}, u32[]{:S(2)}) collective-permute-start(bf16[4,1,128]{2,1,0:T(2,128)(2,1)S(1)} %get-tuple-element.56), channel_id=1, source_target_pairs={{32,0},{64,32},{96,64},{128,96},{160,128},{192,160},{224,192},{256... | collective-permute-start | bytes 3080 | tf_op jit(solution)/shard_map/ppermute | solution.py:34
  70.3 6.2 %collective-permute-start.12 = (bf16[1,6,128]{2,1,0:T(8,128)(2,1)S(1)}, bf16[1,6,128]{2,1,0:T(8,128)(2,1)S(1)}, u32[]{:S(2)}, u32[]{:S(2)}) collective-permute-start(bf16[1,6,128]{2,1,0:T(8,128)(2,1)S(1)} %get-tuple-element.49), channel_id=1, source_target_pairs={{0,1},{1,2},{2,3},{3,4},{4,5},{5,6},{6,7},{7,8},{8,9},{9,10},{10,1... | collective-permute-start | bytes 4616 | tf_op jit(solution)/shard_map/ppermute | solution.py:32
  74.3 7.0 %collective-permute-start.13 = (bf16[1,6,128]{2,1,0:T(8,128)(2,1)S(1)}, bf16[1,6,128]{2,1,0:T(8,128)(2,1)S(1)}, u32[]{:S(2)}, u32[]{:S(2)}) collective-permute-start(bf16[1,6,128]{2,1,0:T(8,128)(2,1)S(1)} %get-tuple-element.50), channel_id=1, source_target_pairs={{1,0},{2,1},{3,2},{4,3},{5,4},{6,5},{7,6},{8,7},{9,8},{10,9},{11,1... | collective-permute-start | bytes 4616 | tf_op jit(solution)/shard_map/ppermute | solution.py:34
  82.8 6.0 %collective-permute-start.14 = (bf16[8,1,128]{2,1,0:T(2,128)(2,1)S(1)}, bf16[8,1,128]{2,1,0:T(2,128)(2,1)S(1)}, u32[]{:S(2)}, u32[]{:S(2)}) collective-permute-start(bf16[8,1,128]{2,1,0:T(2,128)(2,1)S(1)} %get-tuple-element.43), channel_id=1, source_target_pairs={{0,32},{32,64},{64,96},{96,128},{128,160},{160,192},{192,224},{224... | collective-permute-start | bytes 6152 | tf_op jit(solution)/shard_map/ppermute | solution.py:32
  87.3 5.9 %collective-permute-start.15 = (bf16[8,1,128]{2,1,0:T(2,128)(2,1)S(1)}, bf16[8,1,128]{2,1,0:T(2,128)(2,1)S(1)}, u32[]{:S(2)}, u32[]{:S(2)}) collective-permute-start(bf16[8,1,128]{2,1,0:T(2,128)(2,1)S(1)} %get-tuple-element.44), channel_id=1, source_target_pairs={{32,0},{64,32},{96,64},{128,96},{160,128},{192,160},{224,192},{256... | collective-permute-start | bytes 6152 | tf_op jit(solution)/shard_map/ppermute | solution.py:34
  93.2 6.1 %collective-permute-start.16 = (bf16[1,10,128]{2,1,0:T(8,128)(2,1)S(1)}, bf16[1,10,128]{2,1,0:T(8,128)(2,1)S(1)}, u32[]{:S(2)}, u32[]{:S(2)}) collective-permute-start(bf16[1,10,128]{2,1,0:T(8,128)(2,1)S(1)} %get-tuple-element.37), channel_id=1, source_target_pairs={{0,1},{1,2},{2,3},{3,4},{4,5},{5,6},{6,7},{7,8},{8,9},{9,10},{10,1... | collective-permute-start | bytes 7688 | tf_op jit(solution)/shard_map/ppermute | solution.py:32
  97.2 7.0 %collective-permute-start.17 = (bf16[1,10,128]{2,1,0:T(8,128)(2,1)S(1)}, bf16[1,10,128]{2,1,0:T(8,128)(2,1)S(1)}, u32[]{:S(2)}, u32[]{:S(2)}) collective-permute-start(bf16[1,10,128]{2,1,0:T(8,128)(2,1)S(1)} %get-tuple-element.38), channel_id=1, source_target_pairs={{1,0},{2,1},{3,2},{4,3},{5,4},{6,5},{7,6},{8,7},{9,8},{10,9},{11,1... | collective-permute-start | bytes 7688 | tf_op jit(solution)/shard_map/ppermute | solution.py:34
  105.2 5.2 %collective-permute-start.18 = (bf16[8,1,128]{2,1,0:T(2,128)(2,1)S(1)}, bf16[8,1,128]{2,1,0:T(2,128)(2,1)S(1)}, u32[]{:S(2)}, u32[]{:S(2)}) collective-permute-start(bf16[8,1,128]{2,1,0:T(2,128)(2,1)S(1)} %get-tuple-element.41), channel_id=1, source_target_pairs={{0,32},{32,64},{64,96},{96,128},{128,160},{160,192},{192,224},{224... | collective-permute-start | bytes 6152 | tf_op jit(solution)/shard_map/ppermute | solution.py:32
  109.0 5.9 %collective-permute-start.19 = (bf16[8,1,128]{2,1,0:T(2,128)(2,1)S(1)}, bf16[8,1,128]{2,1,0:T(2,128)(2,1)S(1)}, u32[]{:S(2)}, u32[]{:S(2)}) collective-permute-start(bf16[8,1,128]{2,1,0:T(2,128)(2,1)S(1)} %get-tuple-element.42), channel_id=1, source_target_pairs={{32,0},{64,32},{96,64},{128,96},{160,128},{192,160},{224,192},{256... | collective-permute-start | bytes 6152 | tf_op jit(solution)/shard_map/ppermute | solution.py:34
  114.9 6.1 %collective-permute-start.20 = (bf16[1,10,128]{2,1,0:T(8,128)(2,1)S(1)}, bf16[1,10,128]{2,1,0:T(8,128)(2,1)S(1)}, u32[]{:S(2)}, u32[]{:S(2)}) collective-permute-start(bf16[1,10,128]{2,1,0:T(8,128)(2,1)S(1)} %get-tuple-element.33), channel_id=1, source_target_pairs={{0,1},{1,2},{2,3},{3,4},{4,5},{5,6},{6,7},{7,8},{8,9},{9,10},{10,1... | collective-permute-start | bytes 7688 | tf_op jit(solution)/shard_map/ppermute | solution.py:32
  118.9 7.0 %collective-permute-start.21 = (bf16[1,10,128]{2,1,0:T(8,128)(2,1)S(1)}, bf16[1,10,128]{2,1,0:T(8,128)(2,1)S(1)}, u32[]{:S(2)}, u32[]{:S(2)}) collective-permute-start(bf16[1,10,128]{2,1,0:T(8,128)(2,1)S(1)} %get-tuple-element.34), channel_id=1, source_target_pairs={{1,0},{2,1},{3,2},{4,3},{5,4},{6,5},{7,6},{8,7},{9,8},{10,9},{11,1... | collective-permute-start | bytes 7688 | tf_op jit(solution)/shard_map/ppermute | solution.py:34
  128.1 19.1 %all-to-all-start = ((f32[16,1,256]{2,1,0:T(1,128)}), f32[16,1,256]{2,1,0:T(1,128)S(1)}, u32[]{:S(2)}, u32[]{:S(2)}) async-start(f32[16,1,256]{2,1,0:T(1,128)} %reshape.145), calls=%async_computation | async-start | bytes 32768 | tf_op jit(solution)/shard_map/all_to_all | solution.py:17
  149.0 6.1 %collective-permute-start.22 = (bf16[20,1,128]{2,0,1:T(8,128)(2,1)S(1)}, bf16[20,1,128]{2,0,1:T(8,128)(2,1)S(1)}, u32[]{:S(2)}, u32[]{:S(2)}) collective-permute-start(bf16[20,1,128]{2,0,1:T(8,128)(2,1)S(1)} %get-tuple-element.27), channel_id=1, source_target_pairs={{0,1},{1,2},{2,3},{3,4},{4,5},{5,6},{6,7},{7,8},{8,9},{9,10},{10,1... | collective-permute-start | bytes 15368 | tf_op jit(solution)/shard_map/ppermute | solution.py:32
  153.0 7.2 %collective-permute-start.23 = (bf16[20,1,128]{2,0,1:T(8,128)(2,1)S(1)}, bf16[20,1,128]{2,0,1:T(8,128)(2,1)S(1)}, u32[]{:S(2)}, u32[]{:S(2)}) collective-permute-start(bf16[20,1,128]{2,0,1:T(8,128)(2,1)S(1)} %get-tuple-element.28), channel_id=1, source_target_pairs={{1,0},{2,1},{3,2},{4,3},{5,4},{6,5},{7,6},{8,7},{9,8},{10,9},{11,1... | collective-permute-start | bytes 15368 | tf_op jit(solution)/shard_map/ppermute | solution.py:34
  163.3 4.3 %collective-permute-start.24 = (bf16[1,128,128]{2,1,0:T(8,128)(2,1)S(1)}, bf16[1,128,128]{2,1,0:T(8,128)(2,1)S(1)}, u32[]{:S(2)}, u32[]{:S(2)}) collective-permute-start(bf16[1,128,128]{2,1,0:T(8,128)(2,1)S(1)} %get-tuple-element.15), channel_id=1, source_target_pairs={{0,1},{1,2},{2,3},{3,4},{4,5},{5,6},{6,7},{7,8},{8,9},{9,10},{10,1... | collective-permute-start | bytes 98312 | tf_op jit(solution)/shard_map/ppermute | solution.py:32
  165.2 7.3 %collective-permute-start.25 = (bf16[1,128,128]{2,1,0:T(8,128)(2,1)S(1)}, bf16[1,128,128]{2,1,0:T(8,128)(2,1)S(1)}, u32[]{:S(2)}, u32[]{:S(2)}) collective-permute-start(bf16[1,128,128]{2,1,0:T(8,128)(2,1)S(1)} %get-tuple-element.16), channel_id=1, source_target_pairs={{1,0},{2,1},{3,2},{4,3},{5,4},{6,5},{7,6},{8,7},{9,8},{10,9},{11,1... | collective-permute-start | bytes 98312 | tf_op jit(solution)/shard_map/ppermute | solution.py:34
  175.9 4.3 %collective-permute-start.26 = (bf16[1,64,128]{2,1,0:T(8,128)(2,1)S(1)}, bf16[1,64,128]{2,1,0:T(8,128)(2,1)S(1)}, u32[]{:S(2)}, u32[]{:S(2)}) collective-permute-start(bf16[1,64,128]{2,1,0:T(8,128)(2,1)S(1)} %get-tuple-element.23), channel_id=1, source_target_pairs={{0,1},{1,2},{2,3},{3,4},{4,5},{5,6},{6,7},{7,8},{8,9},{9,10},{10,1... | collective-permute-start | bytes 49160 | tf_op jit(solution)/shard_map/ppermute | solution.py:32
  177.9 7.2 %collective-permute-start.27 = (bf16[1,64,128]{2,1,0:T(8,128)(2,1)S(1)}, bf16[1,64,128]{2,1,0:T(8,128)(2,1)S(1)}, u32[]{:S(2)}, u32[]{:S(2)}) collective-permute-start(bf16[1,64,128]{2,1,0:T(8,128)(2,1)S(1)} %get-tuple-element.24), channel_id=1, source_target_pairs={{1,0},{2,1},{3,2},{4,3},{5,4},{6,5},{7,6},{8,7},{9,8},{10,9},{11,1... | collective-permute-start | bytes 49160 | tf_op jit(solution)/shard_map/ppermute | solution.py:34
  187.6 4.5 %collective-permute-start.28 = (bf16[1,64,128]{2,1,0:T(8,128)(2,1)S(1)}, bf16[1,64,128]{2,1,0:T(8,128)(2,1)S(1)}, u32[]{:S(2)}, u32[]{:S(2)}) collective-permute-start(bf16[1,64,128]{2,1,0:T(8,128)(2,1)S(1)} %get-tuple-element.21), channel_id=1, source_target_pairs={{0,1},{1,2},{2,3},{3,4},{4,5},{5,6},{6,7},{7,8},{8,9},{9,10},{10,1... | collective-permute-start | bytes 49160 | tf_op jit(solution)/shard_map/ppermute | solution.py:32
  189.6 7.2 %collective-permute-start.29 = (bf16[1,64,128]{2,1,0:T(8,128)(2,1)S(1)}, bf16[1,64,128]{2,1,0:T(8,128)(2,1)S(1)}, u32[]{:S(2)}, u32[]{:S(2)}) collective-permute-start(bf16[1,64,128]{2,1,0:T(8,128)(2,1)S(1)} %get-tuple-element.22), channel_id=1, source_target_pairs={{1,0},{2,1},{3,2},{4,3},{5,4},{6,5},{7,6},{8,7},{9,8},{10,9},{11,1... | collective-permute-start | bytes 49160 | tf_op jit(solution)/shard_map/ppermute | solution.py:34
  199.4 4.5 %collective-permute-start.30 = (bf16[1,128,128]{2,1,0:T(8,128)(2,1)S(1)}, bf16[1,128,128]{2,1,0:T(8,128)(2,1)S(1)}, u32[]{:S(2)}, u32[]{:S(2)}) collective-permute-start(bf16[1,128,128]{2,1,0:T(8,128)(2,1)S(1)} %get-tuple-element.13), channel_id=1, source_target_pairs={{0,1},{1,2},{2,3},{3,4},{4,5},{5,6},{6,7},{7,8},{8,9},{9,10},{10,1... | collective-permute-start | bytes 98312 | tf_op jit(solution)/shard_map/ppermute | solution.py:32
  201.3 7.5 %collective-permute-start.31 = (bf16[1,128,128]{2,1,0:T(8,128)(2,1)S(1)}, bf16[1,128,128]{2,1,0:T(8,128)(2,1)S(1)}, u32[]{:S(2)}, u32[]{:S(2)}) collective-permute-start(bf16[1,128,128]{2,1,0:T(8,128)(2,1)S(1)} %get-tuple-element.14), channel_id=1, source_target_pairs={{1,0},{2,1},{3,2},{4,3},{5,4},{6,5},{7,6},{8,7},{9,8},{10,9},{11,1... | collective-permute-start | bytes 98312 | tf_op jit(solution)/shard_map/ppermute | solution.py:34
  211.0 4.4 %collective-permute-start.32 = (bf16[1,128,128]{2,1,0:T(8,128)(2,1)S(1)}, bf16[1,128,128]{2,1,0:T(8,128)(2,1)S(1)}, u32[]{:S(2)}, u32[]{:S(2)}) collective-permute-start(bf16[1,128,128]{2,1,0:T(8,128)(2,1)S(1)} %get-tuple-element.11), channel_id=1, source_target_pairs={{0,1},{1,2},{2,3},{3,4},{4,5},{5,6},{6,7},{7,8},{8,9},{9,10},{10,1... | collective-permute-start | bytes 98312 | tf_op jit(solution)/shard_map/ppermute | solution.py:32
  212.9 7.3 %collective-permute-start.33 = (bf16[1,128,128]{2,1,0:T(8,128)(2,1)S(1)}, bf16[1,128,128]{2,1,0:T(8,128)(2,1)S(1)}, u32[]{:S(2)}, u32[]{:S(2)}) collective-permute-start(bf16[1,128,128]{2,1,0:T(8,128)(2,1)S(1)} %get-tuple-element.12), channel_id=1, source_target_pairs={{1,0},{2,1},{3,2},{4,3},{5,4},{6,5},{7,6},{8,7},{9,8},{10,9},{11,1... | collective-permute-start | bytes 98312 | tf_op jit(solution)/shard_map/ppermute | solution.py:34
  222.1 4.5 %collective-permute-start.34 = (bf16[20,1,128]{2,0,1:T(8,128)(2,1)S(1)}, bf16[20,1,128]{2,0,1:T(8,128)(2,1)S(1)}, u32[]{:S(2)}, u32[]{:S(2)}) collective-permute-start(bf16[20,1,128]{2,0,1:T(8,128)(2,1)S(1)} %get-tuple-element.25), channel_id=1, source_target_pairs={{0,1},{1,2},{2,3},{3,4},{4,5},{5,6},{6,7},{7,8},{8,9},{9,10},{10,1... | collective-permute-start | bytes 15368 | tf_op jit(solution)/shard_map/ppermute | solution.py:32
  224.1 7.1 %collective-permute-start.35 = (bf16[20,1,128]{2,0,1:T(8,128)(2,1)S(1)}, bf16[20,1,128]{2,0,1:T(8,128)(2,1)S(1)}, u32[]{:S(2)}, u32[]{:S(2)}) collective-permute-start(bf16[20,1,128]{2,0,1:T(8,128)(2,1)S(1)} %get-tuple-element.26), channel_id=1, source_target_pairs={{1,0},{2,1},{3,2},{4,3},{5,4},{6,5},{7,6},{8,7},{9,8},{10,9},{11,1... | collective-permute-start | bytes 15368 | tf_op jit(solution)/shard_map/ppermute | solution.py:34
  234.2 4.3 %collective-permute-start.36 = (bf16[1,128,128]{2,1,0:T(8,128)(2,1)S(1)}, bf16[1,128,128]{2,1,0:T(8,128)(2,1)S(1)}, u32[]{:S(2)}, u32[]{:S(2)}) collective-permute-start(bf16[1,128,128]{2,1,0:T(8,128)(2,1)S(1)} %get-tuple-element.9), channel_id=1, source_target_pairs={{0,1},{1,2},{2,3},{3,4},{4,5},{5,6},{6,7},{7,8},{8,9},{9,10},{10,1... | collective-permute-start | bytes 98312 | tf_op jit(solution)/shard_map/ppermute | solution.py:32
  236.2 7.3 %collective-permute-start.37 = (bf16[1,128,128]{2,1,0:T(8,128)(2,1)S(1)}, bf16[1,128,128]{2,1,0:T(8,128)(2,1)S(1)}, u32[]{:S(2)}, u32[]{:S(2)}) collective-permute-start(bf16[1,128,128]{2,1,0:T(8,128)(2,1)S(1)} %get-tuple-element.10), channel_id=1, source_target_pairs={{1,0},{2,1},{3,2},{4,3},{5,4},{6,5},{7,6},{8,7},{9,8},{10,9},{11,1... | collective-permute-start | bytes 98312 | tf_op jit(solution)/shard_map/ppermute | solution.py:34
  246.6 4.3 %collective-permute-start.38 = (bf16[1,64,128]{2,1,0:T(8,128)(2,1)S(1)}, bf16[1,64,128]{2,1,0:T(8,128)(2,1)S(1)}, u32[]{:S(2)}, u32[]{:S(2)}) collective-permute-start(bf16[1,64,128]{2,1,0:T(8,128)(2,1)S(1)} %get-tuple-element.19), channel_id=1, source_target_pairs={{0,1},{1,2},{2,3},{3,4},{4,5},{5,6},{6,7},{7,8},{8,9},{9,10},{10,1... | collective-permute-start | bytes 49160 | tf_op jit(solution)/shard_map/ppermute | solution.py:32
  248.5 7.2 %collective-permute-start.39 = (bf16[1,64,128]{2,1,0:T(8,128)(2,1)S(1)}, bf16[1,64,128]{2,1,0:T(8,128)(2,1)S(1)}, u32[]{:S(2)}, u32[]{:S(2)}) collective-permute-start(bf16[1,64,128]{2,1,0:T(8,128)(2,1)S(1)} %get-tuple-element.20), channel_id=1, source_target_pairs={{1,0},{2,1},{3,2},{4,3},{5,4},{6,5},{7,6},{8,7},{9,8},{10,9},{11,1... | collective-permute-start | bytes 49160 | tf_op jit(solution)/shard_map/ppermute | solution.py:34
  257.5 4.5 %collective-permute-start.40 = (bf16[1,64,128]{2,1,0:T(8,128)(2,1)S(1)}, bf16[1,64,128]{2,1,0:T(8,128)(2,1)S(1)}, u32[]{:S(2)}, u32[]{:S(2)}) collective-permute-start(bf16[1,64,128]{2,1,0:T(8,128)(2,1)S(1)} %get-tuple-element.17), channel_id=1, source_target_pairs={{0,1},{1,2},{2,3},{3,4},{4,5},{5,6},{6,7},{7,8},{8,9},{9,10},{10,1... | collective-permute-start | bytes 49160 | tf_op jit(solution)/shard_map/ppermute | solution.py:32
  259.4 7.2 %collective-permute-start.41 = (bf16[1,64,128]{2,1,0:T(8,128)(2,1)S(1)}, bf16[1,64,128]{2,1,0:T(8,128)(2,1)S(1)}, u32[]{:S(2)}, u32[]{:S(2)}) collective-permute-start(bf16[1,64,128]{2,1,0:T(8,128)(2,1)S(1)} %get-tuple-element.18), channel_id=1, source_target_pairs={{1,0},{2,1},{3,2},{4,3},{5,4},{6,5},{7,6},{8,7},{9,8},{10,9},{11,1... | collective-permute-start | bytes 49160 | tf_op jit(solution)/shard_map/ppermute | solution.py:34
  269.2 4.3 %collective-permute-start.42 = (bf16[1,128,128]{2,1,0:T(8,128)(2,1)S(1)}, bf16[1,128,128]{2,1,0:T(8,128)(2,1)S(1)}, u32[]{:S(2)}, u32[]{:S(2)}) collective-permute-start(bf16[1,128,128]{2,1,0:T(8,128)(2,1)S(1)} %get-tuple-element.7), channel_id=1, source_target_pairs={{0,1},{1,2},{2,3},{3,4},{4,5},{5,6},{6,7},{7,8},{8,9},{9,10},{10,1... | collective-permute-start | bytes 98312 | tf_op jit(solution)/shard_map/ppermute | solution.py:32
  271.1 7.3 %collective-permute-start.43 = (bf16[1,128,128]{2,1,0:T(8,128)(2,1)S(1)}, bf16[1,128,128]{2,1,0:T(8,128)(2,1)S(1)}, u32[]{:S(2)}, u32[]{:S(2)}) collective-permute-start(bf16[1,128,128]{2,1,0:T(8,128)(2,1)S(1)} %get-tuple-element.8), channel_id=1, source_target_pairs={{1,0},{2,1},{3,2},{4,3},{5,4},{6,5},{7,6},{8,7},{9,8},{10,9},{11,1... | collective-permute-start | bytes 98312 | tf_op jit(solution)/shard_map/ppermute | solution.py:34
  280.7 4.3 %collective-permute-start.44 = (bf16[1,128,128]{2,1,0:T(8,128)(2,1)S(1)}, bf16[1,128,128]{2,1,0:T(8,128)(2,1)S(1)}, u32[]{:S(2)}, u32[]{:S(2)}) collective-permute-start(bf16[1,128,128]{2,1,0:T(8,128)(2,1)S(1)} %get-tuple-element.5), channel_id=1, source_target_pairs={{0,1},{1,2},{2,3},{3,4},{4,5},{5,6},{6,7},{7,8},{8,9},{9,10},{10,1... | collective-permute-start | bytes 98312 | tf_op jit(solution)/shard_map/ppermute | solution.py:32
  282.6 7.3 %collective-permute-start.45 = (bf16[1,128,128]{2,1,0:T(8,128)(2,1)S(1)}, bf16[1,128,128]{2,1,0:T(8,128)(2,1)S(1)}, u32[]{:S(2)}, u32[]{:S(2)}) collective-permute-start(bf16[1,128,128]{2,1,0:T(8,128)(2,1)S(1)} %get-tuple-element.6), channel_id=1, source_target_pairs={{1,0},{2,1},{3,2},{4,3},{5,4},{6,5},{7,6},{8,7},{9,8},{10,9},{11,1... | collective-permute-start | bytes 98312 | tf_op jit(solution)/shard_map/ppermute | solution.py:34
  (13 other events, 93.1 us)
